TPU v7x, 256 devices: a whole 4x4x8 slice. The times are simulated.
256 devices in a mesh: seq: 4 (over y), ch: 64 (over x, z, core).
Axes of the slice: x: 4, y: 4, z: 8, core: 2. Of those that a mesh axis runs over, the one named last changes fastest.
Arguments:
- tokens: bfloat16 [1024, 8192], P('seq', 'ch'), may hold values from -6 to 6
- in_weight: bfloat16 [8192, 3, 8192], P(None, None, 'ch'), may hold values from -0.0625 to 0.0625
- short_taps: float32 [3, 3, 8192], P(None, None, 'ch'), may hold values from -3 to 3
- decay_rates: float32 [16, 512], P(None, 'ch'), may hold values from 0.05 to 200
- residues: float32 [16, 512], P(None, 'ch'), may hold values from -0.18 to 0.18
- out_weight: bfloat16 [8192, 8192], P('ch'), may hold values from -0.1875 to 0.1875
Outputs:
- mixed: bfloat16 [1024, 8192], P('seq', 'ch')
All inputs are finite; a program needn't handle non-finite values.
Results may differ from a plain program's by a relative error of at most 0.007.
Values may be sent and summed in bfloat16 or wider, within the bound.
No kernel may reach another device: no remote copies, remote signals or barrier semaphores. Data moves between devices by JAX's collectives and lax.ppermute only.
A program may use at most 64 MiB of HBM per device.

v0:
```python
import math

import jax
import jax.numpy as jnp
from jax import lax
from jax.sharding import PartitionSpec as P

TAPS = 3


def passed_along(block, axis, distance):
    devices = range(lax.axis_size(axis))
    route = [(i - distance, i) for i in devices if i - distance in devices]
    return lax.ppermute(block, axis, route)


def on_device(tokens, in_weight, short_taps, decay_rates, residues, out_weight):
    rows_here = tokens.shape[0]
    width_here = in_weight.shape[2]
    model_width = in_weight.shape[0]
    filter_count = decay_rates.shape[1]
    mode_count = decay_rates.shape[0]
    group_width = width_here // filter_count
    tokens_all = rows_here * lax.axis_size("seq")
    flat_weight = in_weight.reshape(model_width, 3 * width_here)
    gathered = lax.all_gather(tokens, "ch", axis=1, tiled=True)
    projected = jnp.dot(gathered, flat_weight, preferred_element_type=jnp.float32).astype(
        jnp.bfloat16
    )
    previous = passed_along(projected[rows_here - (TAPS - 1) :], "seq", 1)
    padded = jnp.concatenate([previous, projected], axis=0).astype(jnp.float32)
    flat_taps = short_taps.reshape(TAPS, 3 * width_here)
    filtered = jnp.zeros((rows_here, 3 * width_here), jnp.float32)
    for shift_back in range(TAPS):
        filtered = (
            filtered
            + flat_taps[shift_back]
            * padded[TAPS - 1 - shift_back : TAPS - 1 - shift_back + rows_here]
        )
    query_stream = filtered[:, :width_here]
    gated_in = filtered[:, width_here : 2 * width_here] * filtered[:, 2 * width_here :]
    block_len = math.gcd(rows_here, 128)
    block_count = rows_here // block_len
    scaled_rates = decay_rates / tokens_all
    offsets_in = jnp.arange(block_len, dtype=jnp.float32)
    filter_taps = jnp.sum(
        residues[None] * jnp.exp(-scaled_rates[None] * offsets_in[:, None, None]), axis=1
    )
    distance = jnp.arange(block_len)[:, None] - jnp.arange(block_len)[None, :]
    lookup = jnp.maximum(distance, 0)
    toeplitz = jnp.where((distance >= 0)[None], filter_taps.T[:, lookup], 0.0)
    blocks_in = gated_in.reshape(block_count, block_len, filter_count, group_width)
    local_part = jnp.einsum("gts,bsgi->btgi", toeplitz, blocks_in, precision=lax.Precision.HIGHEST)
    end_weights = jnp.exp(-scaled_rates[:, :, None] * (block_len - 1 - offsets_in)[None, None, :])
    block_ends = jnp.einsum(
        "mgs,bsgi->bmgi", end_weights, blocks_in, precision=lax.Precision.HIGHEST
    )
    inner_decay = jnp.exp(-scaled_rates * block_len)[:, :, None]
    running = jnp.zeros((mode_count, filter_count, group_width), jnp.float32)
    starts_list = []
    for block_number in range(block_count):
        starts_list.append(running)
        running = inner_decay * running + block_ends[block_number]
    local_starts = jnp.stack(starts_list, axis=0)
    end_state = running.reshape(mode_count, width_here)
    block_decay = jnp.repeat(jnp.exp(-scaled_rates * rows_here), group_width, axis=1)
    incoming = jnp.zeros((mode_count, width_here), jnp.float32)
    for hop_number in range(lax.axis_size("seq") - 1):
        incoming = passed_along(end_state + block_decay * incoming, "seq", 1)
    block_offsets = (jnp.arange(block_count, dtype=jnp.float32) * block_len)[:, None, None]
    start_decay = jnp.exp(-scaled_rates[None] * block_offsets)
    block_starts = (
        local_starts
        + start_decay[..., None] * incoming.reshape(mode_count, filter_count, group_width)[None]
    )
    carry_weights = residues[None] * jnp.exp(
        -scaled_rates[None] * (offsets_in + 1.0)[:, None, None]
    )
    carried = jnp.einsum(
        "tmg,bmgi->btgi", carry_weights, block_starts, precision=lax.Precision.HIGHEST
    )
    convolved = (local_part + carried).reshape(rows_here, width_here)
    gated_out = (query_stream * convolved).astype(jnp.bfloat16)
    turned = lax.psum_scatter(
        lax.dot_general(
            out_weight, gated_out, (((0,), (1,)), ((), ())), preferred_element_type=jnp.float32
        ),
        "ch",
        scatter_dimension=0,
        tiled=True,
    )
    mixed = turned.T.astype(jnp.bfloat16)
    return mixed


def solution(mesh):
    in_specs = (
        P("seq", "ch"),
        P(None, None, "ch"),
        P(None, None, "ch"),
        P(None, "ch"),
        P(None, "ch"),
        P("ch", None),
    )
    out_specs = P("seq", "ch")
    return jax.shard_map(
        on_device, mesh=mesh, in_specs=in_specs, out_specs=out_specs, check_vma=False
    )
```

profile of v0, /device:TPU:24, one launch (start us, length us, event | category | flops | bytes accessed | tf_op | source)
XLA Modules:
  0.0 342.3 jit_solution(9144535828070933124)
XLA Ops:
  6.5 0.7 all-gather.2.cloned.1.call-update
  7.3 8.8 %copy.18 = bf16[8192,3,128]{0,2,1:T(8,128)(2,1)} copy(bf16[8192,3,128]{2,0,1:T(8,128)(2,1)} %param.7) | data formatting | bytes 12582912 | tf_op args[1]
  16.1 0.1 multiply_reduce_fusion
  16.4 72.2 %all-gather.2.cloned.1.call-done = bf16[256,8192]{1,0:T(8,128)(2,1)} async-done(((bf16[256,128]{1,0:T(8,128)(2,1)}), bf16[256,8192]{1,0:T(8,128)(2,1)}) %all-gather.2.cloned.1.call-update) | async-done | bytes 4194320 | tf_op jit(solution)/shard_map/all_gather | solution.py:26
  88.6 6.4 %convolution_convert_fusion = bf16[256,384]{1,0:T(8,128)(2,1)S(1)} fusion(bf16[256,8192]{1,0:T(8,128)(2,1)} %all-gather.2.cloned.1.call-done, bf16[8192,384]{0,1:T(8,128)(2,1)} %bitcast.77), kind=kOutput, calls=%fused_computation.2 | convolution fusion | flops 1610711040 | bytes 10682368 | tf_op jit(solution)/shard_map/dot_general | solution.py:27
  95.0 1.3 collective-permute-start
  96.3 4.2 %collective-permute-done = bf16[2,384]{1,0:T(2,128)(2,1)S(1)} collective-permute-done((bf16[2,384]{1,0:T(2,128)(2,1)S(1)}, bf16[2,384]{1,0:T(2,128)(2,1)S(1)}, u32[]{:S(2)}, u32[]{:S(2)}) %collective-permute-start) | collective-permute-done | bytes 1568 | tf_op jit(solution)/shard_map/ppermute | solution.py:14
  100.6 0.1 fusion.4
  100.7 0.1 copy.19
  100.9 0.3 convolution_bitcast_fusion.1
  101.3 1.3 collective-permute-start.1
  102.6 4.8 %collective-permute-done.1 = f32[16,128]{0,1:T(8,128)S(1)} collective-permute-done((f32[16,128]{0,1:T(8,128)S(1)}, f32[16,128]{0,1:T(8,128)S(1)}, u32[]{:S(2)}, u32[]{:S(2)}) %collective-permute-start.1) | collective-permute-done | bytes 8224 | tf_op jit(solution)/shard_map/ppermute | solution.py:14
  107.4 1.3 collective-permute-start.2
  108.8 0.1 copy.20
  108.9 54.8 %gather_fusion = f32[16384,8]{1,0:T(8,128)} fusion(f32[8,128]{0,1:T(8,128)S(1)} %bitcast.75, s32[16384]{0:T(1024)S(1)} %bitcast_clamp_fusion), kind=kCustom, calls=%fused_computation | custom fusion | bytes 1114112 | tf_op jit(solution)/shard_map/gather | solution.py:51
  163.6 5.1 %copy.21 = f32[128,128,8]{1,0,2:T(8,128)S(1)} copy(f32[128,128,8]{2,1,0:T(8,128)} %bitcast.76) | data formatting | bytes 1048576 | tf_op jit(solution)/shard_map/gather | solution.py:51
  168.8 1.3 collective-permute-start.3
  170.1 0.9 fusion.1
  171.0 4.6 %collective-permute-done.3 = f32[16,128]{0,1:T(8,128)S(1)} collective-permute-done((f32[16,128]{0,1:T(8,128)S(1)}, f32[16,128]{0,1:T(8,128)S(1)}, u32[]{:S(2)}, u32[]{:S(2)}) %collective-permute-start.3) | collective-permute-done | bytes 8224 | tf_op jit(solution)/shard_map/ppermute | solution.py:14
  175.6 0.3 fusion
  176.0 0.1 copy.25
  176.1 4.5 %convolution_bitcast_fusion = f32[8192,256]{0,1:T(8,128)} fusion(bf16[128,8192]{1,0:T(8,128)(2,1)S(1)} %copy-done, f32[256,128]{1,0:T(8,128)S(1)} %copy.25, f32[256,384]{1,0:T(8,128)S(1)} %fusion.4), kind=kOutput, calls=%fused_computation.1 | convolution fusion | flops 536936448 | bytes 10747904 | tf_op jit(solution)/shard_map/dot_general | solution.py:85
  180.6 153.3 %reduce-scatter.2.cloned.1.call-done = f32[128,256]{0,1:T(8,128)} async-done(((f32[8192,256]{0,1:T(8,128)}), f32[128,256]{0,1:T(8,128)}) %reduce-scatter.2.cloned.1.call-update) | async-done | bytes 131088 | tf_op jit(solution)/shard_map/reduce_scatter | solution.py:84
  333.9 1.5 convert_bitcast_fusion
  (30 shorter events, 0.5 us)
Async XLA Ops:
  6.5 169.6 %copy-start = (bf16[128,8192]{1,0:T(8,128)(2,1)S(1)}, bf16[128,8192]{1,0:T(8,128)(2,1)}, u32[]{:S(2)}) copy-start(bf16[128,8192]{1,0:T(8,128)(2,1)} %param.11) | copy-start | bytes 6291460
  6.5 82.1 %all-gather.2.cloned.1.call-start = ((), (), s32[]{:S(2)}) async-start(), calls=%async_computation.1 | async-start | bytes 4259840 | tf_op jit(solution)/shard_map/all_gather | solution.py:26
  7.3 8.8 %copy-start.3 = (f32[16,8]{0,1:T(8,128)S(1)}, f32[16,8]{0,1:T(8,128)}, u32[]{:S(2)}) copy-start(f32[16,8]{0,1:T(8,128)} %param.9) | copy-start | bytes 1540
  7.3 8.9 %copy-start.2 = (f32[16,8]{0,1:T(8,128)S(1)}, f32[16,8]{0,1:T(8,128)}, u32[]{:S(2)}) copy-start(f32[16,8]{0,1:T(8,128)} %param.10) | copy-start | bytes 1540
  7.3 9.0 %copy-start.1 = (f32[3,3,128]{2,1,0:T(4,128)S(1)}, f32[3,3,128]{2,1,0:T(4,128)}, u32[]{:S(2)}) copy-start(f32[3,3,128]{2,1,0:T(4,128)} %param.8) | copy-start | bytes 13828
  7.3 326.6 %reduce-scatter.2.cloned.1.call-start = ((), (), s32[]{:S(2)}) async-start(), calls=%async_computation.2 | async-start | bytes 8519680 | tf_op jit(solution)/shard_map/reduce_scatter | solution.py:84
  95.0 5.5 %collective-permute-start = (bf16[2,384]{1,0:T(2,128)(2,1)S(1)}, bf16[2,384]{1,0:T(2,128)(2,1)S(1)}, u32[]{:S(2)}, u32[]{:S(2)}) collective-permute-start(bf16[2,384]{1,0:T(2,128)(2,1)S(1)} %slice.53), channel_id=1, source_target_pairs={{0,64},{64,128},{128,192},{1,65},{65,129},{129,193},{2,66},{66,130... | collective-permute-start | bytes 4616 | tf_op jit(solution)/shard_map/ppermute | solution.py:14
  101.3 6.2 %collective-permute-start.1 = (f32[16,128]{0,1:T(8,128)S(1)}, f32[16,128]{0,1:T(8,128)S(1)}, u32[]{:S(2)}, u32[]{:S(2)}) collective-permute-start(f32[16,128]{0,1:T(8,128)S(1)} %get-tuple-element.5), channel_id=1, source_target_pairs={{0,64},{64,128},{128,192},{1,65},{65,129},{129,193},{2,66},{66,130... | collective-permute-start | bytes 24584 | tf_op jit(solution)/shard_map/ppermute | solution.py:14
  107.4 61.3 %collective-permute-start.2 = (f32[16,128]{0,1:T(8,128)S(1)}, f32[16,128]{0,1:T(8,128)S(1)}, u32[]{:S(2)}, u32[]{:S(2)}) collective-permute-start(f32[16,128]{0,1:T(8,128)S(1)} %fusion.15), channel_id=1, source_target_pairs={{0,64},{64,128},{128,192},{1,65},{65,129},{129,193},{2,66},{66,130... | collective-permute-start | bytes 24584 | tf_op jit(solution)/shard_map/ppermute | solution.py:14
  168.8 6.8 %collective-permute-start.3 = (f32[16,128]{0,1:T(8,128)S(1)}, f32[16,128]{0,1:T(8,128)S(1)}, u32[]{:S(2)}, u32[]{:S(2)}) collective-permute-start(f32[16,128]{0,1:T(8,128)S(1)} %fusion.16), channel_id=1, source_target_pairs={{0,64},{64,128},{128,192},{1,65},{65,129},{129,193},{2,66},{66,130... | collective-permute-start | bytes 24584 | tf_op jit(solution)/shard_map/ppermute | solution.py:14
Sparse Core Ops, SparseCore 0:
  9.9 78.6 all-gather.1
  180.7 153.1 reduce-scatter.1
where the time goes:
time: 343 us; the launch traced here: 342 us
  waiting for transfers between devices  240 us (70%)
  local copies, waits for them, and re-layouts  69.1 us (20%)
  between operations  13.7 us (4%)
  matrix products  12.4 us (4%)
  starting transfers between devices  5.21 us (2%)
    reduce_scatter x1, waiting for transfers between devices, on_device(): lax.psum_scatter(lax.dot_general(out_weight, gated_out, (((0,), (1,)), ((...  153 us
    all_gather x1, waiting for transfers between devices, on_device(): gathered = lax.all_gather(tokens, 'ch', axis=1, tiled=True)  72.2 us
    gather x2, local copies, waits for them, and re-layouts, on_device(): toeplitz = jnp.where((distance >= 0)[None], filter_taps.T[:, lookup], 0.0)  59.9 us
    ppermute x4, waiting for transfers between devices, passed_along(): return lax.ppermute(block, axis, route)  13.6 us
    unnamed x10, local copies, waits for them, and re-layouts  8.78 us
  transfers between devices with their start and end apart: 6, of which 5 were waited for; matrix products, arithmetic and copies ran while one was open for 20% of the time, Pallas kernels for 0%

commit v1 on v0

--- a/solution.py
+++ b/solution.py
@@ -43,12 +43,13 @@
     block_count = rows_here // block_len
     scaled_rates = decay_rates / tokens_all
     offsets_in = jnp.arange(block_len, dtype=jnp.float32)
-    filter_taps = jnp.sum(
-        residues[None] * jnp.exp(-scaled_rates[None] * offsets_in[:, None, None]), axis=1
+    distance = jnp.arange(block_len)[:, None] - jnp.arange(block_len)[None, :]
+    lag = jnp.maximum(distance, 0).astype(jnp.float32)
+    toeplitz = jnp.where(
+        (distance >= 0)[None],
+        jnp.sum(residues[:, :, None, None] * jnp.exp(-scaled_rates[:, :, None, None] * lag), axis=0),
+        0.0,
     )
-    distance = jnp.arange(block_len)[:, None] - jnp.arange(block_len)[None, :]
-    lookup = jnp.maximum(distance, 0)
-    toeplitz = jnp.where((distance >= 0)[None], filter_taps.T[:, lookup], 0.0)
     blocks_in = gated_in.reshape(block_count, block_len, filter_count, group_width)
     local_part = jnp.einsum("gts,bsgi->btgi", toeplitz, blocks_in, precision=lax.Precision.HIGHEST)
     end_weights = jnp.exp(-scaled_rates[:, :, None] * (block_len - 1 - offsets_in)[None, None, :])
@@ -63,10 +64,10 @@
         running = inner_decay * running + block_ends[block_number]
     local_starts = jnp.stack(starts_list, axis=0)
     end_state = running.reshape(mode_count, width_here)
-    block_decay = jnp.repeat(jnp.exp(-scaled_rates * rows_here), group_width, axis=1)
     incoming = jnp.zeros((mode_count, width_here), jnp.float32)
-    for hop_number in range(lax.axis_size("seq") - 1):
-        incoming = passed_along(end_state + block_decay * incoming, "seq", 1)
+    for hops in range(1, lax.axis_size("seq")):
+        decayed = jnp.repeat(jnp.exp(-scaled_rates * (rows_here * (hops - 1))), group_width, axis=1)
+        incoming = incoming + decayed * passed_along(end_state, "seq", hops)
     block_offsets = (jnp.arange(block_count, dtype=jnp.float32) * block_len)[:, None, None]
     start_decay = jnp.exp(-scaled_rates[None] * block_offsets)
     block_starts = (

time: 343 us -> 280 us (0.82)
  local copies, waits for them, and re-layouts: 69.1 us -> 9.26 us
  waiting for transfers between devices: 240 us -> 235 us
    gather x2 -> x0, local copies, waits for them, and re-layouts: 59.9 us -> none  [on_device(): toeplitz = jnp.where((distance >= 0)[None], filter_taps.T[:, lookup], 0.0)]
    unnamed x10 -> x11, local copies, waits for them, and re-layouts: 8.78 us -> 8.84 us
  transfers between devices with their start and end apart: 6 -> 6, of which waited for: 5 -> 6; matrix products, arithmetic and copies ran while one was open for 20% -> 4% of each run, Pallas kernels for 0% -> 0%
where the time goes in v1:
time: 280 us
  waiting for transfers between devices  235 us (84%)
  between operations  13.6 us (5%)
  matrix products  12.4 us (4%)
  local copies, waits for them, and re-layouts  9.26 us (3%)
  starting transfers between devices  5.21 us (2%)
  other arithmetic  3.89 us (1%)
    reduce_scatter x1, waiting for transfers between devices, on_device(): lax.psum_scatter(lax.dot_general(out_weight, gated_out, (((0,), (1,)), ((...  152 us
    all_gather x1, waiting for transfers between devices, on_device(): gathered = lax.all_gather(tokens, 'ch', axis=1, tiled=True)  70.2 us
    ppermute x4, waiting for transfers between devices, passed_along(): return lax.ppermute(block, axis, route)  12.3 us
    unnamed x11, local copies, waits for them, and re-layouts  8.84 us
    dot_general x1, matrix products, on_device(): jnp.dot(gathered, flat_weight, preferred_element_type=jnp.float32)  6.41 us
  transfers between devices with their start and end apart: 6, of which 6 were waited for; matrix products, arithmetic and copies ran while one was open for 4% of the time, Pallas kernels for 0%

profile of v1, /device:TPU:24, one launch (start us, length us, event | category | flops | bytes accessed | tf_op | source)
XLA Modules:
  0.0 279.5 jit_solution(7239117187040444387)
XLA Ops:
  6.5 0.7 all-gather.2.cloned.1.call-update
  7.3 8.7 %copy.20 = bf16[8192,3,128]{0,2,1:T(8,128)(2,1)} copy(bf16[8192,3,128]{2,0,1:T(8,128)(2,1)} %param.7) | data formatting | bytes 12582912 | tf_op args[1]
  16.3 0.1 multiply_exponential_fusion
  16.4 2.0 multiply_reduce_fusion
  18.4 70.2 %all-gather.2.cloned.1.call-done = bf16[256,8192]{1,0:T(8,128)(2,1)} async-done(((bf16[256,128]{1,0:T(8,128)(2,1)}), bf16[256,8192]{1,0:T(8,128)(2,1)}) %all-gather.2.cloned.1.call-update) | async-done | bytes 4194320 | tf_op jit(solution)/shard_map/all_gather | solution.py:26
  88.6 6.4 %convolution_convert_fusion = bf16[256,384]{1,0:T(8,128)(2,1)S(1)} fusion(bf16[256,8192]{1,0:T(8,128)(2,1)} %all-gather.2.cloned.1.call-done, bf16[8192,384]{0,1:T(8,128)(2,1)} %bitcast.69), kind=kOutput, calls=%fused_computation.2 | convolution fusion | flops 1610711040 | bytes 10682368 | tf_op jit(solution)/shard_map/dot_general | solution.py:27
  95.0 1.3 collective-permute-start
  96.3 4.2 %collective-permute-done = bf16[2,384]{1,0:T(2,128)(2,1)S(1)} collective-permute-done((bf16[2,384]{1,0:T(2,128)(2,1)S(1)}, bf16[2,384]{1,0:T(2,128)(2,1)S(1)}, u32[]{:S(2)}, u32[]{:S(2)}) %collective-permute-start) | collective-permute-done | bytes 1568 | tf_op jit(solution)/shard_map/ppermute | solution.py:14
  100.6 0.1 fusion.3
  100.7 0.1 copy.21
  100.9 0.3 convolution_bitcast_fusion.1
  101.3 1.3 collective-permute-start.1
  102.6 1.3 collective-permute-start.2
  103.9 1.3 collective-permute-start.3
  105.2 2.2 collective-permute-done.1
  107.4 2.8 %collective-permute-done.2 = f32[16,128]{0,1:T(8,128)S(1)} collective-permute-done((f32[16,128]{0,1:T(8,128)S(1)}, f32[16,128]{0,1:T(8,128)S(1)}, u32[]{:S(2)}, u32[]{:S(2)}) %collective-permute-start.2) | collective-permute-done | bytes 8224 | tf_op jit(solution)/shard_map/ppermute | solution.py:14
  110.2 3.1 %collective-permute-done.3 = f32[16,128]{0,1:T(8,128)S(1)} collective-permute-done((f32[16,128]{0,1:T(8,128)S(1)}, f32[16,128]{0,1:T(8,128)S(1)}, u32[]{:S(2)}, u32[]{:S(2)}) %collective-permute-start.3) | collective-permute-done | bytes 8224 | tf_op jit(solution)/shard_map/ppermute | solution.py:14
  113.3 0.3 fusion.8
  113.7 0.9 fusion
  114.6 0.1 copy.26
  114.7 0.1 copy.27
  114.8 4.5 %convolution_bitcast_fusion = f32[8192,256]{0,1:T(8,128)} fusion(bf16[128,8192]{1,0:T(8,128)(2,1)S(1)} %copy-done, f32[256,128]{1,0:T(8,128)S(1)} %copy.27, f32[256,384]{1,0:T(8,128)S(1)} %fusion.3), kind=kOutput, calls=%fused_computation | convolution fusion | flops 536936448 | bytes 10747904 | tf_op jit(solution)/shard_map/dot_general | solution.py:86
  119.3 151.8 %reduce-scatter.2.cloned.1.call-done = f32[128,256]{0,1:T(8,128)} async-done(((f32[8192,256]{0,1:T(8,128)}), f32[128,256]{0,1:T(8,128)}) %reduce-scatter.2.cloned.1.call-update) | async-done | bytes 131088 | tf_op jit(solution)/shard_map/reduce_scatter | solution.py:85
  271.1 1.5 convert_bitcast_fusion
  (28 shorter events, 0.5 us)
Async XLA Ops:
  6.5 108.3 %copy-start = (bf16[128,8192]{1,0:T(8,128)(2,1)S(1)}, bf16[128,8192]{1,0:T(8,128)(2,1)}, u32[]{:S(2)}) copy-start(bf16[128,8192]{1,0:T(8,128)(2,1)} %param.11) | copy-start | bytes 6291460
  6.5 82.1 %all-gather.2.cloned.1.call-start = ((), (), s32[]{:S(2)}) async-start(), calls=%async_computation.1 | async-start | bytes 4259840 | tf_op jit(solution)/shard_map/all_gather | solution.py:26
  7.3 8.8 %copy-start.3 = (f32[16,8]{0,1:T(8,128)S(1)}, f32[16,8]{0,1:T(8,128)}, u32[]{:S(2)}) copy-start(f32[16,8]{0,1:T(8,128)} %param.9) | copy-start | bytes 1540
  7.3 8.9 %copy-start.1 = (f32[16,8]{0,1:T(8,128)S(1)}, f32[16,8]{0,1:T(8,128)}, u32[]{:S(2)}) copy-start(f32[16,8]{0,1:T(8,128)} %param.10) | copy-start | bytes 1540
  7.3 9.0 %copy-start.2 = (f32[3,3,128]{2,1,0:T(4,128)S(1)}, f32[3,3,128]{2,1,0:T(4,128)}, u32[]{:S(2)}) copy-start(f32[3,3,128]{2,1,0:T(4,128)} %param.8) | copy-start | bytes 13828
  7.3 263.8 %reduce-scatter.2.cloned.1.call-start = ((), (), s32[]{:S(2)}) async-start(), calls=%async_computation.2 | async-start | bytes 8519680 | tf_op jit(solution)/shard_map/reduce_scatter | solution.py:85
  95.0 5.5 %collective-permute-start = (bf16[2,384]{1,0:T(2,128)(2,1)S(1)}, bf16[2,384]{1,0:T(2,128)(2,1)S(1)}, u32[]{:S(2)}, u32[]{:S(2)}) collective-permute-start(bf16[2,384]{1,0:T(2,128)(2,1)S(1)} %slice.51), channel_id=1, source_target_pairs={{0,64},{64,128},{128,192},{1,65},{65,129},{129,193},{2,66},{66,130... | collective-permute-start | bytes 4616 | tf_op jit(solution)/shard_map/ppermute | solution.py:14
  101.3 6.2 %collective-permute-start.1 = (f32[16,128]{0,1:T(8,128)S(1)}, f32[16,128]{0,1:T(8,128)S(1)}, u32[]{:S(2)}, u32[]{:S(2)}) collective-permute-start(f32[16,128]{0,1:T(8,128)S(1)} %bitcast_add_fusion), channel_id=1, source_target_pairs={{0,64},{64,128},{128,192},{1,65},{65,129},{129,193},{2,66},{66,130... | collective-permute-start | bytes 24584 | tf_op jit(solution)/shard_map/ppermute | solution.py:14
  102.6 7.7 %collective-permute-start.2 = (f32[16,128]{0,1:T(8,128)S(1)}, f32[16,128]{0,1:T(8,128)S(1)}, u32[]{:S(2)}, u32[]{:S(2)}) collective-permute-start(f32[16,128]{0,1:T(8,128)S(1)} %bitcast_add_fusion), channel_id=1, source_target_pairs={{0,128},{64,192},{1,129},{65,193},{2,130},{66,194},{3,131},{67,195... | collective-permute-start | bytes 24584 | tf_op jit(solution)/shard_map/ppermute | solution.py:14
  103.9 9.4 %collective-permute-start.3 = (f32[16,128]{0,1:T(8,128)S(1)}, f32[16,128]{0,1:T(8,128)S(1)}, u32[]{:S(2)}, u32[]{:S(2)}) collective-permute-start(f32[16,128]{0,1:T(8,128)S(1)} %bitcast_add_fusion), channel_id=1, source_target_pairs={{0,192},{1,193},{2,194},{3,195},{4,196},{5,197},{6,198},{7,199},{8... | collective-permute-start | bytes 24584 | tf_op jit(solution)/shard_map/ppermute | solution.py:14
Sparse Core Ops, SparseCore 0:
  9.9 78.6 all-gather.1
  119.4 151.6 reduce-scatter.1

commit v2 on v1

--- a/solution.py
+++ b/solution.py
@@ -3,7 +3,7 @@
 import jax
 import jax.numpy as jnp
 from jax import lax
-from jax.sharding import PartitionSpec as P
+from jax.sharding import Mesh, PartitionSpec as P
 
 TAPS = 3
 
@@ -12,6 +12,33 @@
     devices = range(lax.axis_size(axis))
     route = [(i - distance, i) for i in devices if i - distance in devices]
     return lax.ppermute(block, axis, route)
+
+
+CH = ("x", "z", "core")
+
+
+def gather_features(tokens):
+    rows, width = tokens.shape
+    chips = lax.axis_size(("x", "z"))
+    spread = jnp.broadcast_to(tokens[None], (chips,) + tokens.shape)
+    same_core = lax.all_to_all(spread, ("x", "z"), 0, 0, tiled=True)
+    both = jnp.broadcast_to(same_core[None], (2,) + same_core.shape)
+    every = lax.all_to_all(both, "core", 0, 0, tiled=True)
+    return every.transpose(2, 1, 0, 3).reshape(rows, 2 * chips * width)
+
+
+def summed_over(parts, axis):
+    got = lax.all_to_all(parts.astype(jnp.bfloat16), axis, 0, 0, tiled=True)
+    return jnp.sum(got.astype(jnp.float32), axis=0)
+
+
+def sum_over_channels(partial):
+    nx, nz = lax.axis_size("x"), lax.axis_size("z")
+    width = partial.shape[0] // (nx * nz * 2)
+    arranged = partial.reshape(nx, nz, 2, width, partial.shape[1]).transpose(2, 0, 1, 3, 4)
+    by_core = summed_over(arranged, "core")
+    by_x = summed_over(by_core, "x")
+    return summed_over(by_x, "z")
 
 
 def on_device(tokens, in_weight, short_taps, decay_rates, residues, out_weight):
@@ -23,7 +50,7 @@
     group_width = width_here // filter_count
     tokens_all = rows_here * lax.axis_size("seq")
     flat_weight = in_weight.reshape(model_width, 3 * width_here)
-    gathered = lax.all_gather(tokens, "ch", axis=1, tiled=True)
+    gathered = gather_features(tokens)
     projected = jnp.dot(gathered, flat_weight, preferred_element_type=jnp.float32).astype(
         jnp.bfloat16
     )
@@ -82,28 +109,33 @@
     )
     convolved = (local_part + carried).reshape(rows_here, width_here)
     gated_out = (query_stream * convolved).astype(jnp.bfloat16)
-    turned = lax.psum_scatter(
+    turned = sum_over_channels(
         lax.dot_general(
             out_weight, gated_out, (((0,), (1,)), ((), ())), preferred_element_type=jnp.float32
-        ),
-        "ch",
-        scatter_dimension=0,
-        tiled=True,
+        )
     )
     mixed = turned.T.astype(jnp.bfloat16)
     return mixed
 
 
+def fine_mesh(mesh):
+    devices = mesh.devices
+    coords = [d.coords for d in devices.flat]
+    nx = len({c[0] for c in coords})
+    nz = len({c[2] for c in coords})
+    return Mesh(devices.reshape(devices.shape[0], nx, nz, devices.shape[1] // (nx * nz)), ("seq",) + CH)
+
+
 def solution(mesh):
     in_specs = (
-        P("seq", "ch"),
-        P(None, None, "ch"),
-        P(None, None, "ch"),
-        P(None, "ch"),
-        P(None, "ch"),
-        P("ch", None),
+        P("seq", CH),
+        P(None, None, CH),
+        P(None, None, CH),
+        P(None, CH),
+        P(None, CH),
+        P(CH, None),
     )
-    out_specs = P("seq", "ch")
+    out_specs = P("seq", CH)
     return jax.shard_map(
-        on_device, mesh=mesh, in_specs=in_specs, out_specs=out_specs, check_vma=False
+        on_device, mesh=fine_mesh(mesh), in_specs=in_specs, out_specs=out_specs, check_vma=False
     )

time: 280 us -> 181 us (0.65)
  waiting for transfers between devices: 235 us -> 51.3 us
  blocking collectives: 0 us -> 66.8 us
  local copies, waits for them, and re-layouts: 9.26 us -> 28.2 us
  between operations: 13.6 us -> 0.3 us
  starting transfers between devices: 5.21 us -> 16.6 us
  other arithmetic: 3.89 us -> 10.1 us
  matrix products: 12.4 us -> 7.12 us
    reduce_scatter x1 -> x0, waiting for transfers between devices: 152 us -> none  [on_device(): lax.psum_scatter(lax.dot_general(out_weight, gated_out, (((0,), (1,)), ((...]
    all_gather x1 -> x0, waiting for transfers between devices: 70.2 us -> none  [on_device(): gathered = lax.all_gather(tokens, 'ch', axis=1, tiled=True)]
    all_to_all x0 -> x4, blocking collectives: none -> 66.8 us  [the longest x3 59.4 us: summed_over(): got = lax.all_to_all(parts.astype(jnp.bfloat16), axis, 0, 0, tiled=True)]
    all_to_all x0 -> x1, waiting for transfers between devices: none -> 39 us  [gather_features(): same_core = lax.all_to_all(spread, ('x', 'z'), 0, 0, tiled=True)]
    all_to_all x0 -> x1, starting transfers between devices: none -> 11.4 us  [gather_features(): same_core = lax.all_to_all(spread, ('x', 'z'), 0, 0, tiled=True)]
    convert_element_type x0 -> x2, local copies, waits for them, and re-layouts: none -> 10.6 us  [summed_over(): got = lax.all_to_all(parts.astype(jnp.bfloat16), axis, 0, 0, tiled=True)]
    reduce_sum x0 -> x3, other arithmetic: none -> 7.79 us  [summed_over(): return jnp.sum(got.astype(jnp.float32), axis=0)]
    dot_general x1, matrix products: 6.41 us -> 2.38 us  [on_device(): jnp.dot(gathered, flat_weight, preferred_element_type=jnp.float32)]
  transfers between devices with their start and end apart: 6 -> 5, of which waited for: 6 -> 5; matrix products, arithmetic and copies ran while one was open for 4% -> 6% of each run, Pallas kernels for 0% -> 0%
where the time goes in v2:
time: 181 us; the launch traced here: 180 us
  blocking collectives  66.8 us (37%)
  waiting for transfers between devices  51.3 us (28%)
  local copies, waits for them, and re-layouts  28.2 us (16%)
  starting transfers between devices  16.6 us (9%)
  other arithmetic  10.1 us (6%)
  matrix products  7.12 us (4%)
    all_to_all x3, blocking collectives, summed_over(): got = lax.all_to_all(parts.astype(jnp.bfloat16), axis, 0, 0, tiled=True)  59.4 us
    all_to_all x1, waiting for transfers between devices, gather_features(): same_core = lax.all_to_all(spread, ('x', 'z'), 0, 0, tiled=True)  39 us
    ppermute x4, waiting for transfers between devices, passed_along(): return lax.ppermute(block, axis, route)  12.3 us
    all_to_all x1, starting transfers between devices, gather_features(): same_core = lax.all_to_all(spread, ('x', 'z'), 0, 0, tiled=True)  11.4 us
    unnamed x16, local copies, waits for them, and re-layouts  11 us
    convert_element_type x2, local copies, waits for them, and re-layouts, summed_over(): got = lax.all_to_all(parts.astype(jnp.bfloat16), axis, 0, 0, tiled=True)  10.6 us
    reduce_sum x3, other arithmetic, summed_over(): return jnp.sum(got.astype(jnp.float32), axis=0)  7.79 us
    all_to_all x1, blocking collectives, gather_features(): every = lax.all_to_all(both, 'core', 0, 0, tiled=True)  7.37 us
  transfers between devices with their start and end apart: 5, of which 5 were waited for; matrix products, arithmetic and copies ran while one was open for 6% of the time, Pallas kernels for 0%

profile of v2, /device:TPU:24, one launch (start us, length us, event | category | flops | bytes accessed | tf_op | source)
XLA Modules:
  0.0 180.4 jit_solution(7650180378157730479)
XLA Ops:
  1.1 1.6 broadcast_in_dim.24
  2.7 11.4 %all-to-all-start = ((bf16[32,256,128]{1,2,0:T(8,128)(2,1)}), bf16[32,256,128]{1,2,0:T(8,128)(2,1)}, u32[]{:S(2)}, u32[]{:S(2)}) async-start(bf16[32,256,128]{1,2,0:T(8,128)(2,1)} %broadcast_in_dim.24), calls=%async_computation | async-start | bytes 4194304 | tf_op jit(solution)/shard_map/all_to_all | solution.py:24
  14.2 8.7 %copy.64 = bf16[8192,3,128]{0,2,1:T(8,128)(2,1)} copy(bf16[8192,3,128]{2,0,1:T(8,128)(2,1)} %param.7) | data formatting | bytes 12582912 | tf_op args[1]
  23.2 2.0 %multiply_reduce_fusion = f32[8,128,128]{2,1,0:T(8,128)S(1)} fusion(f32[128,128]{1,0:T(8,128)S(1)} %maximum_convert_fusion.1, f32[16,8]{1,0:T(8,128)S(1)} %copy.67, f32[16,8]{1,0:T(8,128)S(1)} %copy.66), kind=kLoop, calls=%fused_computation.2 | loop fusion | flops 6160384 | bytes 590848 | tf_op jit(solution)/shard_map/reduce_sum | solution.py:77
  25.2 39.0 %all-to-all-done = bf16[32,256,128]{1,2,0:T(8,128)(2,1)} async-done(((bf16[32,256,128]{1,2,0:T(8,128)(2,1)}), bf16[32,256,128]{1,2,0:T(8,128)(2,1)}, u32[]{:S(2)}, u32[]{:S(2)}) %all-to-all-start) | async-done | bytes 2097184 | tf_op jit(solution)/shard_map/all_to_all | solution.py:24
  64.2 2.1 %broadcast_in_dim.25 = bf16[2,32,256,128]{2,3,1,0:T(8,128)(2,1)S(1)} broadcast(bf16[32,256,128]{1,2,0:T(8,128)(2,1)} %all-to-all-done), dimensions={1,2,3} | broadcast | bytes 6291456 | tf_op jit(solution)/shard_map/broadcast_in_dim | solution.py:25
  66.3 7.4 %all_to_all.25 = bf16[2,32,256,128]{2,3,1,0:T(8,128)(2,1)S(1)} all-to-all(bf16[2,32,256,128]{2,3,1,0:T(8,128)(2,1)S(1)} %broadcast_in_dim.25), channel_id=1, replica_groups=mesh['seq'=4,'x'=4,'z'=8,'core'=2] {'core'}, dimensions={0} | all-to-all | bytes 8388608 | tf_op jit(solution)/shard_map/all_to_all | solution.py:26
  75.2 2.4 %convolution_convert_fusion.1 = bf16[256,384]{1,0:T(8,128)(2,1)S(1)} fusion(bf16[256,8192]{0,1:T(8,128)(2,1)S(1)} %bitcast.80, bf16[8192,384]{0,1:T(8,128)(2,1)S(1)} %bitcast.79), kind=kOutput, calls=%fused_computation.4 | convolution fusion | flops 1610711040 | bytes 10682368 | tf_op jit(solution)/shard_map/dot_general | solution.py:54
  77.6 1.3 collective-permute-start
  78.9 4.2 %collective-permute-done = bf16[2,384]{1,0:T(2,128)(2,1)S(1)} collective-permute-done((bf16[2,384]{1,0:T(2,128)(2,1)S(1)}, bf16[2,384]{1,0:T(2,128)(2,1)S(1)}, u32[]{:S(2)}, u32[]{:S(2)}) %collective-permute-start) | collective-permute-done | bytes 1568 | tf_op jit(solution)/shard_map/ppermute | solution.py:14
  83.9 1.3 collective-permute-start.1
  85.2 1.3 collective-permute-start.2
  87.8 2.2 %collective-permute-done.1 = f32[16,128]{0,1:T(8,128)S(1)} collective-permute-done((f32[16,128]{0,1:T(8,128)S(1)}, f32[16,128]{0,1:T(8,128)S(1)}, u32[]{:S(2)}, u32[]{:S(2)}) %collective-permute-start.1) | collective-permute-done | bytes 8224 | tf_op jit(solution)/shard_map/ppermute | solution.py:14
  90.0 2.8 %collective-permute-done.2 = f32[16,128]{0,1:T(8,128)S(1)} collective-permute-done((f32[16,128]{0,1:T(8,128)S(1)}, f32[16,128]{0,1:T(8,128)S(1)}, u32[]{:S(2)}, u32[]{:S(2)}) %collective-permute-start.2) | collective-permute-done | bytes 8224 | tf_op jit(solution)/shard_map/ppermute | solution.py:14
  92.8 3.1 %collective-permute-done.3 = f32[16,128]{0,1:T(8,128)S(1)} collective-permute-done((f32[16,128]{0,1:T(8,128)S(1)}, f32[16,128]{0,1:T(8,128)S(1)}, u32[]{:S(2)}, u32[]{:S(2)}) %collective-permute-start.3) | collective-permute-done | bytes 8224 | tf_op jit(solution)/shard_map/ppermute | solution.py:14
  97.4 3.2 %fusion = bf16[8192,256]{0,1:T(8,128)(2,1)} fusion(bf16[128,8192]{1,0:T(8,128)(2,1)S(1)} %copy-done, f32[256,128]{1,0:T(8,128)S(1)} %copy.71, f32[256,384]{1,0:T(8,128)S(1)} %fusion.4), kind=kOutput, calls=%fused_computation.1 | convolution fusion | flops 539033600 | bytes 6553600 | tf_op jit(solution)/shard_map/dot_general | solution.py:113
  100.6 7.8 %convert_element_type.43 = bf16[4,8,2,128,256]{3,2,1,0,4:T(2,128)(2,1)} reshape(bf16[8192,256]{0,1:T(8,128)(2,1)} %fusion) | data formatting | bytes 8388608 | tf_op jit(solution)/shard_map/convert_element_type | solution.py:31
  108.4 2.8 %copy.89 = bf16[4,8,2,128,256]{3,1,0,4,2:T(8,128)(2,1)S(1)} copy(bf16[4,8,2,128,256]{3,2,1,0,4:T(2,128)(2,1)} %convert_element_type.43) | data formatting | bytes 8388608 | tf_op jit(solution)/shard_map/convert_element_type | solution.py:31
  111.2 8.2 %all_to_all.26 = bf16[2,4,8,128,256]{3,2,1,4,0:T(8,128)(2,1)} all-to-all(bf16[2,4,8,128,256]{3,2,1,4,0:T(8,128)(2,1)S(1)} %bitcast.76), channel_id=1, replica_groups=mesh['seq'=4,'x'=4,'z'=8,'core'=2] {'core'}, dimensions={0} | all-to-all | bytes 8388608 | tf_op jit(solution)/shard_map/all_to_all | solution.py:31
  119.4 4.9 %reduce_sum.46 = bf16[4,8,128,256]{2,1,0,3:T(8,128)(2,1)} reduce(bf16[2,4,8,128,256]{3,2,1,4,0:T(8,128)(2,1)} %all_to_all.26, bf16[]{:T(256)} %constant.24.clone.1), dimensions={0}, to_apply=%region_1.2 | reduce | flops 1048576 | bytes 6291458 | tf_op jit(solution)/shard_map/reduce_sum | solution.py:32
  124.3 2.0 %copy.74 = bf16[4,8,128,256]{2,1,3,0:T(8,128)(2,1)S(1)} copy(bf16[4,8,128,256]{2,1,0,3:T(8,128)(2,1)} %reduce_sum.46) | data formatting | bytes 4194304 | tf_op jit(solution)/shard_map/reduce_sum | solution.py:32
  126.2 30.1 %all_to_all.27 = bf16[4,8,128,256]{2,1,3,0:T(8,128)(2,1)} all-to-all(bf16[4,8,128,256]{2,1,3,0:T(8,128)(2,1)S(1)} %copy.74), channel_id=1, replica_groups=mesh['seq'=4,'x'=4,'z'=8,'core'=2] {'x'}, dimensions={0} | all-to-all | bytes 4194304 | tf_op jit(solution)/shard_map/all_to_all | solution.py:31
  156.3 2.2 %reduce_sum.47 = bf16[8,128,256]{1,0,2:T(8,128)(2,1)S(1)} reduce(bf16[4,8,128,256]{2,1,3,0:T(8,128)(2,1)} %all_to_all.27, bf16[]{:T(256)} %constant.24.clone.1), dimensions={0}, to_apply=%region_2.3 | reduce | flops 786432 | bytes 2621442 | tf_op jit(solution)/shard_map/reduce_sum | solution.py:32
  158.6 21.1 %all_to_all.28 = bf16[8,128,256]{1,2,0:T(8,128)(2,1)S(1)} all-to-all(bf16[8,128,256]{1,2,0:T(8,128)(2,1)S(1)} %copy.76), channel_id=1, replica_groups=mesh['seq'=4,'x'=4,'z'=8,'core'=2] {'z'}, dimensions={0} | all-to-all | bytes 1048576 | tf_op jit(solution)/shard_map/all_to_all | solution.py:31
  (43 shorter events, 7.2 us)
Async XLA Ops:
  0.0 97.4 %copy-start = (bf16[128,8192]{1,0:T(8,128)(2,1)S(1)}, bf16[128,8192]{1,0:T(8,128)(2,1)}, u32[]{:S(2)}) copy-start(bf16[128,8192]{1,0:T(8,128)(2,1)} %param.11) | copy-start | bytes 6291460
  2.7 61.5 %all-to-all-start = ((bf16[32,256,128]{1,2,0:T(8,128)(2,1)}), bf16[32,256,128]{1,2,0:T(8,128)(2,1)}, u32[]{:S(2)}, u32[]{:S(2)}) async-start(bf16[32,256,128]{1,2,0:T(8,128)(2,1)} %broadcast_in_dim.24), calls=%async_computation | async-start | bytes 4194304 | tf_op jit(solution)/shard_map/all_to_all | solution.py:24
  14.1 8.7 %copy-start.3 = (f32[16,8]{0,1:T(8,128)S(1)}, f32[16,8]{0,1:T(8,128)}, u32[]{:S(2)}) copy-start(f32[16,8]{0,1:T(8,128)} %param.9) | copy-start | bytes 1540
  14.2 8.8 %copy-start.1 = (f32[16,8]{0,1:T(8,128)S(1)}, f32[16,8]{0,1:T(8,128)}, u32[]{:S(2)}) copy-start(f32[16,8]{0,1:T(8,128)} %param.10) | copy-start | bytes 1540
  14.2 8.9 %copy-start.2 = (f32[3,3,128]{2,1,0:T(4,128)S(1)}, f32[3,3,128]{2,1,0:T(4,128)}, u32[]{:S(2)}) copy-start(f32[3,3,128]{2,1,0:T(4,128)} %param.8) | copy-start | bytes 13828
  66.3 7.9 %slice-start = ((s8[6291456]{0:T(1024)(128)(4,1)}), s8[4194304]{0:T(1024)(128)(4,1)S(1)}, s32[]{:S(2)}) async-start(s8[6291456]{0:T(1024)(128)(4,1)} %bitcast.77), calls=%async_computation.5 | async-start | bytes 8388608
  73.6 1.6 slice-start.1
  77.6 5.5 %collective-permute-start = (bf16[2,384]{1,0:T(2,128)(2,1)S(1)}, bf16[2,384]{1,0:T(2,128)(2,1)S(1)}, u32[]{:S(2)}, u32[]{:S(2)}) collective-permute-start(bf16[2,384]{1,0:T(2,128)(2,1)S(1)} %slice.51), channel_id=1, source_target_pairs={{0,64},{64,128},{128,192},{1,65},{65,129},{129,193},{2,66},{66,130... | collective-permute-start | bytes 4616 | tf_op jit(solution)/shard_map/ppermute | solution.py:14
  83.9 6.2 %collective-permute-start.1 = (f32[16,128]{0,1:T(8,128)S(1)}, f32[16,128]{0,1:T(8,128)S(1)}, u32[]{:S(2)}, u32[]{:S(2)}) collective-permute-start(f32[16,128]{0,1:T(8,128)S(1)} %bitcast_add_fusion), channel_id=1, source_target_pairs={{0,64},{64,128},{128,192},{1,65},{65,129},{129,193},{2,66},{66,130... | collective-permute-start | bytes 24584 | tf_op jit(solution)/shard_map/ppermute | solution.py:14
  85.2 7.7 %collective-permute-start.2 = (f32[16,128]{0,1:T(8,128)S(1)}, f32[16,128]{0,1:T(8,128)S(1)}, u32[]{:S(2)}, u32[]{:S(2)}) collective-permute-start(f32[16,128]{0,1:T(8,128)S(1)} %bitcast_add_fusion), channel_id=1, source_target_pairs={{0,128},{64,192},{1,129},{65,193},{2,130},{66,194},{3,131},{67,195... | collective-permute-start | bytes 24584 | tf_op jit(solution)/shard_map/ppermute | solution.py:14
  86.5 9.4 %collective-permute-start.3 = (f32[16,128]{0,1:T(8,128)S(1)}, f32[16,128]{0,1:T(8,128)S(1)}, u32[]{:S(2)}, u32[]{:S(2)}) collective-permute-start(f32[16,128]{0,1:T(8,128)S(1)} %bitcast_add_fusion), channel_id=1, source_target_pairs={{0,192},{1,193},{2,194},{3,195},{4,196},{5,197},{6,198},{7,199},{8... | collective-permute-start | bytes 24584 | tf_op jit(solution)/shard_map/ppermute | solution.py:14

commit v3 on v2

--- a/solution.py
+++ b/solution.py
@@ -32,12 +32,24 @@
     return jnp.sum(got.astype(jnp.float32), axis=0)
 
 
+def pair_rows(out_weight):
+    rows, model_width = out_weight.shape
+    nx, nz = lax.axis_size("x"), lax.axis_size("z")
+    width = model_width // (nx * nz * 2)
+    split = out_weight.reshape(rows, nx, nz, 2, width).transpose(3, 0, 1, 2, 4)
+    return lax.all_to_all(split, "core", 0, 0, tiled=True)
+
+
+def project_out(weight_pair, gated_out):
+    both = jnp.broadcast_to(gated_out[None], (2,) + gated_out.shape)
+    inputs_pair = lax.all_to_all(both, "core", 0, 0, tiled=True)
+    return jnp.einsum(
+        "crxzw,ctr->xzwt", weight_pair, inputs_pair, preferred_element_type=jnp.float32
+    )
+
+
 def sum_over_channels(partial):
-    nx, nz = lax.axis_size("x"), lax.axis_size("z")
-    width = partial.shape[0] // (nx * nz * 2)
-    arranged = partial.reshape(nx, nz, 2, width, partial.shape[1]).transpose(2, 0, 1, 3, 4)
-    by_core = summed_over(arranged, "core")
-    by_x = summed_over(by_core, "x")
+    by_x = summed_over(partial, "x")
     return summed_over(by_x, "z")
 
 
@@ -50,6 +62,7 @@
     group_width = width_here // filter_count
     tokens_all = rows_here * lax.axis_size("seq")
     flat_weight = in_weight.reshape(model_width, 3 * width_here)
+    out_weight_pair = pair_rows(out_weight)
     gathered = gather_features(tokens)
     projected = jnp.dot(gathered, flat_weight, preferred_element_type=jnp.float32).astype(
         jnp.bfloat16
@@ -109,11 +122,7 @@
     )
     convolved = (local_part + carried).reshape(rows_here, width_here)
     gated_out = (query_stream * convolved).astype(jnp.bfloat16)
-    turned = sum_over_channels(
-        lax.dot_general(
-            out_weight, gated_out, (((0,), (1,)), ((), ())), preferred_element_type=jnp.float32
-        )
-    )
+    turned = sum_over_channels(project_out(out_weight_pair, gated_out))
     mixed = turned.T.astype(jnp.bfloat16)
     return mixed
 

time: 181 us -> 161 us (0.89)
  waiting for transfers between devices: 51.3 us -> 43.3 us
  other arithmetic: 10.1 us -> 3.44 us
  local copies, waits for them, and re-layouts: 28.2 us -> 22.9 us
  blocking collectives: 66.8 us -> 62.4 us
  starting transfers between devices: 16.6 us -> 20.2 us
    convert_element_type x2 -> x0, local copies, waits for them, and re-layouts: 10.6 us -> none  [summed_over(): got = lax.all_to_all(parts.astype(jnp.bfloat16), axis, 0, 0, tiled=True)]
    all_to_all x3 -> x2, blocking collectives: 59.4 us -> 50.4 us  [summed_over(): got = lax.all_to_all(parts.astype(jnp.bfloat16), axis, 0, 0, tiled=True)]
    all_to_all x1, waiting for transfers between devices: 39 us -> 31 us  [gather_features(): same_core = lax.all_to_all(spread, ('x', 'z'), 0, 0, tiled=True)]
    reduce_sum x3 -> x2, other arithmetic: 7.79 us -> 1.08 us  [summed_over(): return jnp.sum(got.astype(jnp.float32), axis=0)]
    transpose x0 -> x1, local copies, waits for them, and re-layouts: none -> 3.96 us  [pair_rows(): split = out_weight.reshape(rows, nx, nz, 2, width).transpose(3, 0, 1, 2, 4)]
    all_to_all x0 -> x1, blocking collectives: none -> 3.84 us  [project_out(): inputs_pair = lax.all_to_all(both, 'core', 0, 0, tiled=True)]
    all_to_all x0 -> x1, starting transfers between devices: none -> 3.76 us  [pair_rows(): return lax.all_to_all(split, 'core', 0, 0, tiled=True)]
    dot_general x1, matrix products: 2.38 us -> 5.27 us  [on_device(): jnp.dot(gathered, flat_weight, preferred_element_type=jnp.float32)]
  transfers between devices with their start and end apart: 5 -> 6, of which waited for: 5 -> 5; matrix products, arithmetic and copies ran while one was open for 6% -> 18% of each run, Pallas kernels for 0% -> 0%
where the time goes in v3:
time: 161 us; the launch traced here: 160 us
  blocking collectives  62.4 us (39%)
  waiting for transfers between devices  43.3 us (27%)
  local copies, waits for them, and re-layouts  22.9 us (14%)
  starting transfers between devices  20.2 us (13%)
  matrix products  7.56 us (5%)
  other arithmetic  3.44 us (2%)
    all_to_all x2, blocking collectives, summed_over(): got = lax.all_to_all(parts.astype(jnp.bfloat16), axis, 0, 0, tiled=True)  50.4 us
    all_to_all x1, waiting for transfers between devices, gather_features(): same_core = lax.all_to_all(spread, ('x', 'z'), 0, 0, tiled=True)  31 us
    unnamed x11, local copies, waits for them, and re-layouts  13.8 us
    ppermute x4, waiting for transfers between devices, passed_along(): return lax.ppermute(block, axis, route)  12.3 us
    all_to_all x1, starting transfers between devices, gather_features(): same_core = lax.all_to_all(spread, ('x', 'z'), 0, 0, tiled=True)  11.3 us
    all_to_all x1, blocking collectives, gather_features(): every = lax.all_to_all(both, 'core', 0, 0, tiled=True)  8.17 us
    dot_general x1, matrix products, on_device(): jnp.dot(gathered, flat_weight, preferred_element_type=jnp.float32)  5.27 us
    ppermute x4, starting transfers between devices, passed_along(): return lax.ppermute(block, axis, route)  5.17 us
  transfers between devices with their start and end apart: 6, of which 5 were waited for; matrix products, arithmetic and copies ran while one was open for 18% of the time, Pallas kernels for 0%

profile of v3, /device:TPU:24, one launch (start us, length us, event | category | flops | bytes accessed | tf_op | source)
XLA Modules:
  0.0 160.1 jit_solution(3460115919573818336)
XLA Ops:
  0.0 0.9 copy.36
  0.9 1.6 broadcast_in_dim.26
  2.5 11.3 %all-to-all-start = ((bf16[32,256,128]{1,2,0:T(8,128)(2,1)}), bf16[32,256,128]{1,2,0:T(8,128)(2,1)S(1)}, u32[]{:S(2)}, u32[]{:S(2)}) async-start(bf16[32,256,128]{1,2,0:T(8,128)(2,1)} %broadcast_in_dim.26), calls=%async_computation | async-start | bytes 4194304 | tf_op jit(solution)/shard_map/all_to_all | solution.py:24
  13.9 8.7 %copy.38 = bf16[8192,3,128]{0,2,1:T(8,128)(2,1)} copy(bf16[8192,3,128]{2,0,1:T(8,128)(2,1)} %param.7) | data formatting | bytes 12582912 | tf_op args[1]
  22.8 4.1 %copy.46 = bf16[128,8192]{0,1:T(8,128)(2,1)} copy(bf16[128,8192]{1,0:T(8,128)(2,1)} %param.11) | data formatting | bytes 4194304 | tf_op args[5]
  26.8 4.0 %copy.47 = bf16[2,128,4,8,128]{4,1,3,2,0:T(8,128)(2,1)} copy(bf16[2,128,4,8,128]{1,4,0,3,2:T(8,128)(2,1)} %bitcast.88) | data formatting | bytes 4194304 | tf_op jit(solution)/shard_map/transpose | solution.py:39
  30.9 2.0 %multiply_reduce_fusion = f32[8,128,128]{2,1,0:T(8,128)S(1)} fusion(f32[128,128]{1,0:T(8,128)S(1)} %maximum_convert_fusion.1, f32[16,8]{1,0:T(8,128)S(1)} %copy.41, f32[16,8]{1,0:T(8,128)S(1)} %copy.40), kind=kLoop, calls=%fused_computation | loop fusion | flops 6160384 | bytes 590848 | tf_op jit(solution)/shard_map/reduce_sum | solution.py:90
  32.9 31.0 %all-to-all-done = bf16[32,256,128]{1,2,0:T(8,128)(2,1)S(1)} async-done(((bf16[32,256,128]{1,2,0:T(8,128)(2,1)}), bf16[32,256,128]{1,2,0:T(8,128)(2,1)S(1)}, u32[]{:S(2)}, u32[]{:S(2)}) %all-to-all-start) | async-done | bytes 2097184 | tf_op jit(solution)/shard_map/all_to_all | solution.py:24
  64.6 8.2 %all_to_all.30 = bf16[2,32,256,128]{2,3,1,0:T(8,128)(2,1)} all-to-all(bf16[2,32,256,128]{2,3,1,0:T(8,128)(2,1)S(1)} %broadcast_in_dim.27), channel_id=1, replica_groups=mesh['seq'=4,'x'=4,'z'=8,'core'=2] {'core'}, dimensions={0} | all-to-all | bytes 8388608 | tf_op jit(solution)/shard_map/all_to_all | solution.py:26
  72.8 3.8 %all-to-all-start.3 = ((bf16[2,128,4,8,128]{4,1,3,2,0:T(8,128)(2,1)}), bf16[2,128,4,8,128]{4,1,3,2,0:T(8,128)(2,1)S(1)}, u32[]{:S(2)}, u32[]{:S(2)}) async-start(bf16[2,128,4,8,128]{4,1,3,2,0:T(8,128)(2,1)} %copy.47), calls=%async_computation.3 | async-start | bytes 4194304 | tf_op jit(solution)/shard_map/all_to_all | solution.py:40
  76.5 2.5 %copy.37 = bf16[2,32,256,128]{2,3,0,1:T(8,128)(2,1)S(1)} copy(bf16[2,32,256,128]{2,3,1,0:T(8,128)(2,1)} %all_to_all.30) | data formatting | bytes 8388608 | tf_op jit(solution)/shard_map/all_to_all | solution.py:26
  79.0 5.3 %convolution_convert_fusion = bf16[256,384]{1,0:T(8,128)(2,1)S(1)} fusion(bf16[256,8192]{0,1:T(8,128)(2,1)S(1)} %bitcast.90, bf16[8192,384]{0,1:T(8,128)(2,1)} %bitcast.89), kind=kOutput, calls=%fused_computation.3 | convolution fusion | flops 1610711040 | bytes 10682368 | tf_op jit(solution)/shard_map/dot_general | solution.py:67
  84.3 1.3 collective-permute-start
  85.6 4.2 %collective-permute-done = bf16[2,384]{1,0:T(2,128)(2,1)S(1)} collective-permute-done((bf16[2,384]{1,0:T(2,128)(2,1)S(1)}, bf16[2,384]{1,0:T(2,128)(2,1)S(1)}, u32[]{:S(2)}, u32[]{:S(2)}) %collective-permute-start) | collective-permute-done | bytes 1568 | tf_op jit(solution)/shard_map/ppermute | solution.py:14
  90.5 1.3 collective-permute-start.1
  91.8 1.3 collective-permute-start.2
  93.1 1.3 collective-permute-start.3
  94.4 2.2 %collective-permute-done.1 = f32[16,128]{0,1:T(8,128)S(1)} collective-permute-done((f32[16,128]{0,1:T(8,128)S(1)}, f32[16,128]{0,1:T(8,128)S(1)}, u32[]{:S(2)}, u32[]{:S(2)}) %collective-permute-start.1) | collective-permute-done | bytes 8224 | tf_op jit(solution)/shard_map/ppermute | solution.py:14
  96.7 2.8 %collective-permute-done.2 = f32[16,128]{0,1:T(8,128)S(1)} collective-permute-done((f32[16,128]{0,1:T(8,128)S(1)}, f32[16,128]{0,1:T(8,128)S(1)}, u32[]{:S(2)}, u32[]{:S(2)}) %collective-permute-start.2) | collective-permute-done | bytes 8224 | tf_op jit(solution)/shard_map/ppermute | solution.py:14
  99.5 3.1 %collective-permute-done.3 = f32[16,128]{0,1:T(8,128)S(1)} collective-permute-done((f32[16,128]{0,1:T(8,128)S(1)}, f32[16,128]{0,1:T(8,128)S(1)}, u32[]{:S(2)}, u32[]{:S(2)}) %collective-permute-start.3) | collective-permute-done | bytes 8224 | tf_op jit(solution)/shard_map/ppermute | solution.py:14
  102.9 0.9 fusion.1
  104.1 3.8 %all_to_all.31 = bf16[2,256,128]{2,1,0:T(8,128)(2,1)S(1)} all-to-all(bf16[2,256,128]{2,1,0:T(8,128)(2,1)S(1)} %broadcast_in_dim.34), channel_id=1, replica_groups=mesh['seq'=4,'x'=4,'z'=8,'core'=2] {'core'}, dimensions={0} | all-to-all | bytes 262144 | tf_op jit(solution)/shard_map/all_to_all | solution.py:45
  108.7 29.4 %all_to_all.32 = bf16[4,8,128,256]{2,3,1,0:T(8,128)(2,1)S(1)} all-to-all(bf16[4,8,128,256]{2,3,1,0:T(8,128)(2,1)S(1)} %fusion), channel_id=1, replica_groups=mesh['seq'=4,'x'=4,'z'=8,'core'=2] {'x'}, dimensions={0} | all-to-all | bytes 4194304 | tf_op jit(solution)/shard_map/all_to_all | solution.py:31
  138.5 21.0 %all_to_all.33 = bf16[8,128,256]{1,2,0:T(8,128)(2,1)S(1)} all-to-all(bf16[8,128,256]{1,2,0:T(8,128)(2,1)S(1)} %reduce_sum.34), channel_id=1, replica_groups=mesh['seq'=4,'x'=4,'z'=8,'core'=2] {'z'}, dimensions={0} | all-to-all | bytes 1048576 | tf_op jit(solution)/shard_map/all_to_all | solution.py:31
  (37 shorter events, 4.1 us)
Async XLA Ops:
  2.5 61.4 %all-to-all-start = ((bf16[32,256,128]{1,2,0:T(8,128)(2,1)}), bf16[32,256,128]{1,2,0:T(8,128)(2,1)S(1)}, u32[]{:S(2)}, u32[]{:S(2)}) async-start(bf16[32,256,128]{1,2,0:T(8,128)(2,1)} %broadcast_in_dim.26), calls=%async_computation | async-start | bytes 4194304 | tf_op jit(solution)/shard_map/all_to_all | solution.py:24
  13.9 8.7 %copy-start.2 = (f32[16,8]{0,1:T(8,128)S(1)}, f32[16,8]{0,1:T(8,128)}, u32[]{:S(2)}) copy-start(f32[16,8]{0,1:T(8,128)} %param.9) | copy-start | bytes 1540
  13.9 8.8 %copy-start = (f32[16,8]{0,1:T(8,128)S(1)}, f32[16,8]{0,1:T(8,128)}, u32[]{:S(2)}) copy-start(f32[16,8]{0,1:T(8,128)} %param.10) | copy-start | bytes 1540
  22.7 8.1 %copy-start.1 = (f32[3,3,128]{2,1,0:T(4,128)S(1)}, f32[3,3,128]{2,1,0:T(4,128)}, u32[]{:S(2)}) copy-start(f32[3,3,128]{2,1,0:T(4,128)} %param.8) | copy-start | bytes 13828
  72.8 31.3 %all-to-all-start.3 = ((bf16[2,128,4,8,128]{4,1,3,2,0:T(8,128)(2,1)}), bf16[2,128,4,8,128]{4,1,3,2,0:T(8,128)(2,1)S(1)}, u32[]{:S(2)}, u32[]{:S(2)}) async-start(bf16[2,128,4,8,128]{4,1,3,2,0:T(8,128)(2,1)} %copy.47), calls=%async_computation.3 | async-start | bytes 4194304 | tf_op jit(solution)/shard_map/all_to_all | solution.py:40
  84.3 5.5 %collective-permute-start = (bf16[2,384]{1,0:T(2,128)(2,1)S(1)}, bf16[2,384]{1,0:T(2,128)(2,1)S(1)}, u32[]{:S(2)}, u32[]{:S(2)}) collective-permute-start(bf16[2,384]{1,0:T(2,128)(2,1)S(1)} %slice.51), channel_id=1, source_target_pairs={{0,64},{64,128},{128,192},{1,65},{65,129},{129,193},{2,66},{66,130... | collective-permute-start | bytes 4616 | tf_op jit(solution)/shard_map/ppermute | solution.py:14
  90.5 6.2 %collective-permute-start.1 = (f32[16,128]{0,1:T(8,128)S(1)}, f32[16,128]{0,1:T(8,128)S(1)}, u32[]{:S(2)}, u32[]{:S(2)}) collective-permute-start(f32[16,128]{0,1:T(8,128)S(1)} %bitcast_add_fusion), channel_id=1, source_target_pairs={{0,64},{64,128},{128,192},{1,65},{65,129},{129,193},{2,66},{66,130... | collective-permute-start | bytes 24584 | tf_op jit(solution)/shard_map/ppermute | solution.py:14
  91.8 7.7 %collective-permute-start.2 = (f32[16,128]{0,1:T(8,128)S(1)}, f32[16,128]{0,1:T(8,128)S(1)}, u32[]{:S(2)}, u32[]{:S(2)}) collective-permute-start(f32[16,128]{0,1:T(8,128)S(1)} %bitcast_add_fusion), channel_id=1, source_target_pairs={{0,128},{64,192},{1,129},{65,193},{2,130},{66,194},{3,131},{67,195... | collective-permute-start | bytes 24584 | tf_op jit(solution)/shard_map/ppermute | solution.py:14
  93.1 9.4 %collective-permute-start.3 = (f32[16,128]{0,1:T(8,128)S(1)}, f32[16,128]{0,1:T(8,128)S(1)}, u32[]{:S(2)}, u32[]{:S(2)}) collective-permute-start(f32[16,128]{0,1:T(8,128)S(1)} %bitcast_add_fusion), channel_id=1, source_target_pairs={{0,192},{1,193},{2,194},{3,195},{4,196},{5,197},{6,198},{7,199},{8... | collective-permute-start | bytes 24584 | tf_op jit(solution)/shard_map/ppermute | solution.py:14

commit v4 on v3

--- a/solution.py
+++ b/solution.py
@@ -17,14 +17,15 @@
 CH = ("x", "z", "core")
 
 
+def spread_to(block, axis):
+    count = lax.axis_size(axis)
+    return lax.all_to_all(jnp.broadcast_to(block[None], (count,) + block.shape), axis, 0, 0, tiled=True)
+
+
 def gather_features(tokens):
-    rows, width = tokens.shape
-    chips = lax.axis_size(("x", "z"))
-    spread = jnp.broadcast_to(tokens[None], (chips,) + tokens.shape)
-    same_core = lax.all_to_all(spread, ("x", "z"), 0, 0, tiled=True)
-    both = jnp.broadcast_to(same_core[None], (2,) + same_core.shape)
-    every = lax.all_to_all(both, "core", 0, 0, tiled=True)
-    return every.transpose(2, 1, 0, 3).reshape(rows, 2 * chips * width)
+    rows = tokens.shape[0]
+    every = spread_to(spread_to(spread_to(tokens, "z"), "x"), "core")
+    return every.transpose(3, 1, 2, 0, 4).reshape(rows, -1)
 
 
 def summed_over(parts, axis):

time: 161 us -> 153 us (0.950)
  waiting for transfers between devices: 43.3 us -> 17.9 us
  blocking collectives: 62.4 us -> 86.8 us
  starting transfers between devices: 20.2 us -> 13.2 us
    all_to_all x1 -> x2, blocking collectives: 8.17 us -> 33.9 us  [spread_to(): lax.all_to_all(jnp.broadcast_to(block[None], (count,) + block.shape), axi...]
    all_to_all x1, waiting for transfers between devices: 31 us -> 5.64 us  [spread_to(): lax.all_to_all(jnp.broadcast_to(block[None], (count,) + block.shape), axi...]
    all_to_all x1, starting transfers between devices: 11.3 us -> 4.29 us  [spread_to(): lax.all_to_all(jnp.broadcast_to(block[None], (count,) + block.shape), axi...]
  transfers between devices with their start and end apart: 6 -> 6, of which waited for: 5 -> 5; matrix products, arithmetic and copies ran while one was open for 18% -> 19% of each run, Pallas kernels for 0% -> 0%
where the time goes in v4:
time: 153 us; the launch traced here: 152 us
  blocking collectives  86.8 us (57%)
  local copies, waits for them, and re-layouts  23 us (15%)
  waiting for transfers between devices  17.9 us (12%)
  starting transfers between devices  13.2 us (9%)
  matrix products  7.56 us (5%)
  other arithmetic  3.44 us (2%)
    all_to_all x2, blocking collectives, summed_over(): got = lax.all_to_all(parts.astype(jnp.bfloat16), axis, 0, 0, tiled=True)  49 us
    all_to_all x2, blocking collectives, spread_to(): lax.all_to_all(jnp.broadcast_to(block[None], (count,) + block.shape), axi...  33.9 us
    unnamed x11, local copies, waits for them, and re-layouts  13.8 us
    ppermute x4, waiting for transfers between devices, passed_along(): return lax.ppermute(block, axis, route)  12.3 us
    all_to_all x1, waiting for transfers between devices, spread_to(): lax.all_to_all(jnp.broadcast_to(block[None], (count,) + block.shape), axi...  5.64 us
    dot_general x1, matrix products, on_device(): jnp.dot(gathered, flat_weight, preferred_element_type=jnp.float32)  5.28 us
    ppermute x4, starting transfers between devices, passed_along(): return lax.ppermute(block, axis, route)  5.17 us
    all_to_all x1, starting transfers between devices, spread_to(): lax.all_to_all(jnp.broadcast_to(block[None], (count,) + block.shape), axi...  4.29 us
  transfers between devices with their start and end apart: 6, of which 5 were waited for; matrix products, arithmetic and copies ran while one was open for 19% of the time, Pallas kernels for 0%

profile of v4, /device:TPU:24, one launch (start us, length us, event | category | flops | bytes accessed | tf_op | source)
XLA Modules:
  0.0 152.2 jit_solution(8032013608097858482)
XLA Ops:
  0.0 0.9 copy.36
  1.0 25.8 %all_to_all.35 = bf16[8,256,128]{1,2,0:T(8,128)(2,1)S(1)} all-to-all(bf16[8,256,128]{1,2,0:T(8,128)(2,1)S(1)} %broadcast_in_dim.28), channel_id=1, replica_groups=mesh['seq'=4,'x'=4,'z'=8,'core'=2] {'z'}, dimensions={0} | all-to-all | bytes 1048576 | tf_op jit(solution)/shard_map/all_to_all | solution.py:22
  26.7 1.6 %broadcast_in_dim.29 = bf16[4,8,256,128]{2,3,1,0:T(8,128)(2,1)} broadcast(bf16[8,256,128]{1,2,0:T(8,128)(2,1)S(1)} %all_to_all.35), dimensions={1,2,3} | broadcast | bytes 2621440 | tf_op jit(solution)/shard_map/broadcast_in_dim | solution.py:22
  28.3 4.3 %all-to-all-start.1 = ((bf16[4,8,256,128]{2,3,1,0:T(8,128)(2,1)}), bf16[4,8,256,128]{2,3,1,0:T(8,128)(2,1)S(1)}, u32[]{:S(2)}, u32[]{:S(2)}) async-start(bf16[4,8,256,128]{2,3,1,0:T(8,128)(2,1)} %broadcast_in_dim.29), calls=%async_computation.1 | async-start | bytes 4194304 | tf_op jit(solution)/shard_map/all_to_all | solution.py:22
  32.6 8.7 %copy.38 = bf16[8192,3,128]{0,2,1:T(8,128)(2,1)} copy(bf16[8192,3,128]{2,0,1:T(8,128)(2,1)} %param.7) | data formatting | bytes 12582912 | tf_op args[1]
  41.5 4.1 %copy.46 = bf16[128,8192]{0,1:T(8,128)(2,1)} copy(bf16[128,8192]{1,0:T(8,128)(2,1)} %param.11) | data formatting | bytes 4194304 | tf_op args[5]
  45.6 4.0 %copy.47 = bf16[2,128,4,8,128]{4,1,3,2,0:T(8,128)(2,1)} copy(bf16[2,128,4,8,128]{1,4,0,3,2:T(8,128)(2,1)} %bitcast.88) | data formatting | bytes 4194304 | tf_op jit(solution)/shard_map/transpose | solution.py:40
  49.7 2.0 %multiply_reduce_fusion = f32[8,128,128]{2,1,0:T(8,128)S(1)} fusion(f32[128,128]{1,0:T(8,128)S(1)} %maximum_convert_fusion.1, f32[16,8]{1,0:T(8,128)S(1)} %copy.41, f32[16,8]{1,0:T(8,128)S(1)} %copy.40), kind=kLoop, calls=%fused_computation | loop fusion | flops 6160384 | bytes 590848 | tf_op jit(solution)/shard_map/reduce_sum | solution.py:91
  51.7 5.6 %all-to-all-done.1 = bf16[4,8,256,128]{2,3,1,0:T(8,128)(2,1)S(1)} async-done(((bf16[4,8,256,128]{2,3,1,0:T(8,128)(2,1)}), bf16[4,8,256,128]{2,3,1,0:T(8,128)(2,1)S(1)}, u32[]{:S(2)}, u32[]{:S(2)}) %all-to-all-start.1) | async-done | bytes 2097184 | tf_op jit(solution)/shard_map/all_to_all | solution.py:22
  58.0 8.2 %all_to_all.36 = bf16[2,4,8,256,128]{3,4,2,1,0:T(8,128)(2,1)} all-to-all(bf16[2,4,8,256,128]{3,4,2,1,0:T(8,128)(2,1)S(1)} %broadcast_in_dim.30), channel_id=1, replica_groups=mesh['seq'=4,'x'=4,'z'=8,'core'=2] {'core'}, dimensions={0} | all-to-all | bytes 8388608 | tf_op jit(solution)/shard_map/all_to_all | solution.py:22
  66.2 3.8 %all-to-all-start.4 = ((bf16[2,128,4,8,128]{4,1,3,2,0:T(8,128)(2,1)}), bf16[2,128,4,8,128]{4,1,3,2,0:T(8,128)(2,1)S(1)}, u32[]{:S(2)}, u32[]{:S(2)}) async-start(bf16[2,128,4,8,128]{4,1,3,2,0:T(8,128)(2,1)} %copy.47), calls=%async_computation.4 | async-start | bytes 4194304 | tf_op jit(solution)/shard_map/all_to_all | solution.py:41
  69.9 2.5 %copy.37 = bf16[2,4,8,256,128]{3,4,0,2,1:T(8,128)(2,1)S(1)} copy(bf16[2,4,8,256,128]{3,4,2,1,0:T(8,128)(2,1)} %all_to_all.36) | data formatting | bytes 8388608 | tf_op jit(solution)/shard_map/all_to_all | solution.py:22
  72.4 5.3 %convolution_convert_fusion = bf16[256,384]{1,0:T(8,128)(2,1)S(1)} fusion(bf16[256,8192]{0,1:T(8,128)(2,1)S(1)} %bitcast.90, bf16[8192,384]{0,1:T(8,128)(2,1)} %bitcast.89), kind=kOutput, calls=%fused_computation.3 | convolution fusion | flops 1610711040 | bytes 10682368 | tf_op jit(solution)/shard_map/dot_general | solution.py:68
  77.7 1.3 collective-permute-start
  79.0 4.2 %collective-permute-done = bf16[2,384]{1,0:T(2,128)(2,1)S(1)} collective-permute-done((bf16[2,384]{1,0:T(2,128)(2,1)S(1)}, bf16[2,384]{1,0:T(2,128)(2,1)S(1)}, u32[]{:S(2)}, u32[]{:S(2)}) %collective-permute-start) | collective-permute-done | bytes 1568 | tf_op jit(solution)/shard_map/ppermute | solution.py:14
  83.9 1.3 collective-permute-start.1
  85.2 1.3 collective-permute-start.2
  86.5 1.3 collective-permute-start.3
  87.8 2.2 %collective-permute-done.1 = f32[16,128]{0,1:T(8,128)S(1)} collective-permute-done((f32[16,128]{0,1:T(8,128)S(1)}, f32[16,128]{0,1:T(8,128)S(1)}, u32[]{:S(2)}, u32[]{:S(2)}) %collective-permute-start.1) | collective-permute-done | bytes 8224 | tf_op jit(solution)/shard_map/ppermute | solution.py:14
  90.1 2.8 %collective-permute-done.2 = f32[16,128]{0,1:T(8,128)S(1)} collective-permute-done((f32[16,128]{0,1:T(8,128)S(1)}, f32[16,128]{0,1:T(8,128)S(1)}, u32[]{:S(2)}, u32[]{:S(2)}) %collective-permute-start.2) | collective-permute-done | bytes 8224 | tf_op jit(solution)/shard_map/ppermute | solution.py:14
  92.9 3.1 %collective-permute-done.3 = f32[16,128]{0,1:T(8,128)S(1)} collective-permute-done((f32[16,128]{0,1:T(8,128)S(1)}, f32[16,128]{0,1:T(8,128)S(1)}, u32[]{:S(2)}, u32[]{:S(2)}) %collective-permute-start.3) | collective-permute-done | bytes 8224 | tf_op jit(solution)/shard_map/ppermute | solution.py:14
  97.5 3.8 %all_to_all.37 = bf16[2,256,128]{2,1,0:T(8,128)(2,1)S(1)} all-to-all(bf16[2,256,128]{2,1,0:T(8,128)(2,1)S(1)} %broadcast_in_dim.37), channel_id=1, replica_groups=mesh['seq'=4,'x'=4,'z'=8,'core'=2] {'core'}, dimensions={0} | all-to-all | bytes 262144 | tf_op jit(solution)/shard_map/all_to_all | solution.py:46
  102.1 29.4 %all_to_all.38 = bf16[4,8,128,256]{2,3,1,0:T(8,128)(2,1)S(1)} all-to-all(bf16[4,8,128,256]{2,3,1,0:T(8,128)(2,1)S(1)} %fusion), channel_id=1, replica_groups=mesh['seq'=4,'x'=4,'z'=8,'core'=2] {'x'}, dimensions={0} | all-to-all | bytes 4194304 | tf_op jit(solution)/shard_map/all_to_all | solution.py:32
  131.9 19.6 %all_to_all.39 = bf16[8,128,256]{1,2,0:T(8,128)(2,1)S(1)} all-to-all(bf16[8,128,256]{1,2,0:T(8,128)(2,1)S(1)} %reduce_sum.34), channel_id=1, replica_groups=mesh['seq'=4,'x'=4,'z'=8,'core'=2] {'z'}, dimensions={0} | all-to-all | bytes 1048576 | tf_op jit(solution)/shard_map/all_to_all | solution.py:32
  (39 shorter events, 5.0 us)
Async XLA Ops:
  28.3 29.0 %all-to-all-start.1 = ((bf16[4,8,256,128]{2,3,1,0:T(8,128)(2,1)}), bf16[4,8,256,128]{2,3,1,0:T(8,128)(2,1)S(1)}, u32[]{:S(2)}, u32[]{:S(2)}) async-start(bf16[4,8,256,128]{2,3,1,0:T(8,128)(2,1)} %broadcast_in_dim.29), calls=%async_computation.1 | async-start | bytes 4194304 | tf_op jit(solution)/shard_map/all_to_all | solution.py:22
  32.6 8.7 %copy-start.2 = (f32[16,8]{0,1:T(8,128)S(1)}, f32[16,8]{0,1:T(8,128)}, u32[]{:S(2)}) copy-start(f32[16,8]{0,1:T(8,128)} %param.9) | copy-start | bytes 1540
  32.6 8.8 %copy-start = (f32[16,8]{0,1:T(8,128)S(1)}, f32[16,8]{0,1:T(8,128)}, u32[]{:S(2)}) copy-start(f32[16,8]{0,1:T(8,128)} %param.10) | copy-start | bytes 1540
  41.5 8.1 %copy-start.1 = (f32[3,3,128]{2,1,0:T(4,128)S(1)}, f32[3,3,128]{2,1,0:T(4,128)}, u32[]{:S(2)}) copy-start(f32[3,3,128]{2,1,0:T(4,128)} %param.8) | copy-start | bytes 13828
  66.2 31.3 %all-to-all-start.4 = ((bf16[2,128,4,8,128]{4,1,3,2,0:T(8,128)(2,1)}), bf16[2,128,4,8,128]{4,1,3,2,0:T(8,128)(2,1)S(1)}, u32[]{:S(2)}, u32[]{:S(2)}) async-start(bf16[2,128,4,8,128]{4,1,3,2,0:T(8,128)(2,1)} %copy.47), calls=%async_computation.4 | async-start | bytes 4194304 | tf_op jit(solution)/shard_map/all_to_all | solution.py:41
  77.7 5.5 %collective-permute-start = (bf16[2,384]{1,0:T(2,128)(2,1)S(1)}, bf16[2,384]{1,0:T(2,128)(2,1)S(1)}, u32[]{:S(2)}, u32[]{:S(2)}) collective-permute-start(bf16[2,384]{1,0:T(2,128)(2,1)S(1)} %slice.51), channel_id=1, source_target_pairs={{0,64},{64,128},{128,192},{1,65},{65,129},{129,193},{2,66},{66,130... | collective-permute-start | bytes 4616 | tf_op jit(solution)/shard_map/ppermute | solution.py:14
  83.9 6.2 %collective-permute-start.1 = (f32[16,128]{0,1:T(8,128)S(1)}, f32[16,128]{0,1:T(8,128)S(1)}, u32[]{:S(2)}, u32[]{:S(2)}) collective-permute-start(f32[16,128]{0,1:T(8,128)S(1)} %bitcast_add_fusion), channel_id=1, source_target_pairs={{0,64},{64,128},{128,192},{1,65},{65,129},{129,193},{2,66},{66,130... | collective-permute-start | bytes 24584 | tf_op jit(solution)/shard_map/ppermute | solution.py:14
  85.2 7.7 %collective-permute-start.2 = (f32[16,128]{0,1:T(8,128)S(1)}, f32[16,128]{0,1:T(8,128)S(1)}, u32[]{:S(2)}, u32[]{:S(2)}) collective-permute-start(f32[16,128]{0,1:T(8,128)S(1)} %bitcast_add_fusion), channel_id=1, source_target_pairs={{0,128},{64,192},{1,129},{65,193},{2,130},{66,194},{3,131},{67,195... | collective-permute-start | bytes 24584 | tf_op jit(solution)/shard_map/ppermute | solution.py:14
  86.5 9.4 %collective-permute-start.3 = (f32[16,128]{0,1:T(8,128)S(1)}, f32[16,128]{0,1:T(8,128)S(1)}, u32[]{:S(2)}, u32[]{:S(2)}) collective-permute-start(f32[16,128]{0,1:T(8,128)S(1)} %bitcast_add_fusion), channel_id=1, source_target_pairs={{0,192},{1,193},{2,194},{3,195},{4,196},{5,197},{6,198},{7,199},{8... | collective-permute-start | bytes 24584 | tf_op jit(solution)/shard_map/ppermute | solution.py:14

commit v5 on v4

--- a/solution.py
+++ b/solution.py
@@ -54,6 +54,20 @@
     return summed_over(by_x, "z")
 
 
+def from_earlier_blocks(end_state, block_rates, group_width):
+    blocks = lax.axis_size("seq")
+    here = lax.axis_index("seq")
+    ends = spread_to(end_state, "seq")
+    source = jnp.arange(blocks)
+    between = jnp.maximum(here - 1 - source, 0).astype(jnp.float32)
+    decay = jnp.where(
+        (source < here)[:, None, None],
+        jnp.exp(-block_rates[None] * between[:, None, None]),
+        0.0,
+    )
+    return jnp.sum(jnp.repeat(decay, group_width, axis=2) * ends, axis=0)
+
+
 def on_device(tokens, in_weight, short_taps, decay_rates, residues, out_weight):
     rows_here = tokens.shape[0]
     width_here = in_weight.shape[2]
@@ -105,10 +119,7 @@
         running = inner_decay * running + block_ends[block_number]
     local_starts = jnp.stack(starts_list, axis=0)
     end_state = running.reshape(mode_count, width_here)
-    incoming = jnp.zeros((mode_count, width_here), jnp.float32)
-    for hops in range(1, lax.axis_size("seq")):
-        decayed = jnp.repeat(jnp.exp(-scaled_rates * (rows_here * (hops - 1))), group_width, axis=1)
-        incoming = incoming + decayed * passed_along(end_state, "seq", hops)
+    incoming = from_earlier_blocks(end_state, scaled_rates * rows_here, group_width)
     block_offsets = (jnp.arange(block_count, dtype=jnp.float32) * block_len)[:, None, None]
     start_decay = jnp.exp(-scaled_rates[None] * block_offsets)
     block_starts = (

time: 153 us -> 150 us (0.980)
  matrix products: 7.56 us -> 4.66 us
  local copies, waits for them, and re-layouts: 23 us -> 21 us
    ppermute x4 -> x1, waiting for transfers between devices: 12.3 us -> 4.16 us  [passed_along(): return lax.ppermute(block, axis, route)]
    all_to_all x1 -> x2, waiting for transfers between devices: 5.64 us -> 13.5 us  [spread_to(): lax.all_to_all(jnp.broadcast_to(block[None], (count,) + block.shape), axi...]
    all_to_all x1 -> x2, starting transfers between devices: 4.29 us -> 8.98 us  [spread_to(): lax.all_to_all(jnp.broadcast_to(block[None], (count,) + block.shape), axi...]
    ppermute x4 -> x1, starting transfers between devices: 5.17 us -> 1.29 us  [passed_along(): return lax.ppermute(block, axis, route)]
    dot_general x1, matrix products: 5.28 us -> 2.38 us  [on_device(): jnp.dot(gathered, flat_weight, preferred_element_type=jnp.float32)]
    all_to_all x1, local copies, waits for them, and re-layouts: 2.46 us -> 0.48 us  [spread_to(): lax.all_to_all(jnp.broadcast_to(block[None], (count,) + block.shape), axi...]
    unnamed x11 -> x15, local copies, waits for them, and re-layouts: 13.8 us -> 14.1 us
  transfers between devices with their start and end apart: 6 -> 4, of which waited for: 5 -> 3; matrix products, arithmetic and copies ran while one was open for 19% -> 13% of each run, Pallas kernels for 0% -> 0%
where the time goes in v5:
time: 150 us; the launch traced here: 148 us
  blocking collectives  86 us (57%)
  local copies, waits for them, and re-layouts  21 us (14%)
  waiting for transfers between devices  18.9 us (13%)
  starting transfers between devices  14 us (9%)
  matrix products  4.66 us (3%)
  other arithmetic  3.51 us (2%)
    all_to_all x2, blocking collectives, summed_over(): got = lax.all_to_all(parts.astype(jnp.bfloat16), axis, 0, 0, tiled=True)  49 us
    all_to_all x2, blocking collectives, spread_to(): lax.all_to_all(jnp.broadcast_to(block[None], (count,) + block.shape), axi...  33.1 us
    unnamed x15, local copies, waits for them, and re-layouts  14.1 us
    all_to_all x2, waiting for transfers between devices, spread_to(): lax.all_to_all(jnp.broadcast_to(block[None], (count,) + block.shape), axi...  13.5 us
    all_to_all x2, starting transfers between devices, spread_to(): lax.all_to_all(jnp.broadcast_to(block[None], (count,) + block.shape), axi...  8.98 us
    ppermute x1, waiting for transfers between devices, passed_along(): return lax.ppermute(block, axis, route)  4.16 us
    all_to_all x1, blocking collectives, project_out(): inputs_pair = lax.all_to_all(both, 'core', 0, 0, tiled=True)  3.84 us
    all_to_all x1, starting transfers between devices, pair_rows(): return lax.all_to_all(split, 'core', 0, 0, tiled=True)  3.76 us
  transfers between devices with their start and end apart: 4, of which 3 were waited for; matrix products, arithmetic and copies ran while one was open for 13% of the time, Pallas kernels for 0%

profile of v5, /device:TPU:24, one launch (start us, length us, event | category | flops | bytes accessed | tf_op | source)
XLA Modules:
  0.0 148.5 jit_solution(15285223138710566772)
XLA Ops:
  0.0 0.9 copy.42
  1.0 25.8 %all_to_all.40 = bf16[8,256,128]{1,2,0:T(8,128)(2,1)S(1)} all-to-all(bf16[8,256,128]{1,2,0:T(8,128)(2,1)S(1)} %broadcast_in_dim.34), channel_id=1, replica_groups=mesh['seq'=4,'x'=4,'z'=8,'core'=2] {'z'}, dimensions={0} | all-to-all | bytes 1048576 | tf_op jit(solution)/shard_map/all_to_all | solution.py:22
  26.8 1.6 %broadcast_in_dim.35 = bf16[4,8,256,128]{2,3,1,0:T(8,128)(2,1)} broadcast(bf16[8,256,128]{1,2,0:T(8,128)(2,1)S(1)} %all_to_all.40), dimensions={1,2,3} | broadcast | bytes 2621440 | tf_op jit(solution)/shard_map/broadcast_in_dim | solution.py:22
  28.3 4.3 %all-to-all-start.1 = ((bf16[4,8,256,128]{2,3,1,0:T(8,128)(2,1)}), bf16[4,8,256,128]{2,3,1,0:T(8,128)(2,1)S(1)}, u32[]{:S(2)}, u32[]{:S(2)}) async-start(bf16[4,8,256,128]{2,3,1,0:T(8,128)(2,1)} %broadcast_in_dim.35), calls=%async_computation.1 | async-start | bytes 4194304 | tf_op jit(solution)/shard_map/all_to_all | solution.py:22
  32.7 8.7 %copy.44 = bf16[8192,3,128]{0,2,1:T(8,128)(2,1)} copy(bf16[8192,3,128]{2,0,1:T(8,128)(2,1)} %param.7) | data formatting | bytes 12582912 | tf_op args[1]
  41.9 2.0 %multiply_reduce_fusion = f32[8,128,128]{2,1,0:T(8,128)S(1)} fusion(f32[128,128]{1,0:T(8,128)S(1)} %maximum_convert_fusion.1, f32[16,8]{1,0:T(8,128)S(1)} %copy.47, f32[16,8]{1,0:T(8,128)S(1)} %copy.46), kind=kLoop, calls=%fused_computation | loop fusion | flops 6160384 | bytes 590848 | tf_op jit(solution)/shard_map/reduce_sum | solution.py:105
  43.8 13.5 %all-to-all-done.1 = bf16[4,8,256,128]{2,3,1,0:T(8,128)(2,1)S(1)} async-done(((bf16[4,8,256,128]{2,3,1,0:T(8,128)(2,1)}), bf16[4,8,256,128]{2,3,1,0:T(8,128)(2,1)S(1)}, u32[]{:S(2)}, u32[]{:S(2)}) %all-to-all-start.1) | async-done | bytes 2097184 | tf_op jit(solution)/shard_map/all_to_all | solution.py:22
  57.3 0.7 broadcast_in_dim.36
  58.0 7.4 %all_to_all.41 = bf16[2,4,8,256,128]{3,4,2,1,0:T(8,128)(2,1)S(1)} all-to-all(bf16[2,4,8,256,128]{3,4,2,1,0:T(8,128)(2,1)S(1)} %broadcast_in_dim.36), channel_id=1, replica_groups=mesh['seq'=4,'x'=4,'z'=8,'core'=2] {'core'}, dimensions={0} | all-to-all | bytes 8388608 | tf_op jit(solution)/shard_map/all_to_all | solution.py:22
  65.9 1.1 slice-done.1
  67.0 2.4 %convolution_convert_fusion = bf16[256,384]{1,0:T(8,128)(2,1)S(1)} fusion(bf16[256,8192]{0,1:T(8,128)(2,1)S(1)} %bitcast.80, bf16[8192,384]{0,1:T(8,128)(2,1)S(1)} %bitcast.79), kind=kOutput, calls=%fused_computation.3 | convolution fusion | flops 1610711040 | bytes 10682368 | tf_op jit(solution)/shard_map/dot_general | solution.py:82
  69.4 1.3 collective-permute-start
  70.7 4.2 %collective-permute-done = bf16[2,384]{1,0:T(2,128)(2,1)S(1)} collective-permute-done((bf16[2,384]{1,0:T(2,128)(2,1)S(1)}, bf16[2,384]{1,0:T(2,128)(2,1)S(1)}, u32[]{:S(2)}, u32[]{:S(2)}) %collective-permute-start) | collective-permute-done | bytes 1568 | tf_op jit(solution)/shard_map/ppermute | solution.py:14
  76.3 4.7 %all-to-all-start.3 = ((f32[4,16,128]{2,1,0:T(8,128)}), f32[4,16,128]{2,1,0:T(8,128)S(1)}, u32[]{:S(2)}, u32[]{:S(2)}) async-start(f32[4,16,128]{2,1,0:T(8,128)} %broadcast_in_dim.47), calls=%async_computation.3 | async-start | bytes 65536 | tf_op jit(solution)/shard_map/all_to_all | solution.py:22
  81.3 3.2 %copy.55 = bf16[128,8192]{0,1:T(8,128)(2,1)S(1)} copy(bf16[128,8192]{1,0:T(8,128)(2,1)} %param.11) | data formatting | bytes 4194304 | tf_op args[5]
  84.5 2.6 %copy.56 = bf16[2,128,4,8,128]{4,1,3,2,0:T(8,128)(2,1)} copy(bf16[2,128,4,8,128]{1,4,0,3,2:T(8,128)(2,1)S(1)} %bitcast.76) | data formatting | bytes 4194304 | tf_op jit(solution)/shard_map/transpose | solution.py:40
  87.1 3.8 %all-to-all-start.5 = ((bf16[2,128,4,8,128]{4,1,3,2,0:T(8,128)(2,1)}), bf16[2,128,4,8,128]{4,1,3,2,0:T(8,128)(2,1)S(1)}, u32[]{:S(2)}, u32[]{:S(2)}) async-start(bf16[2,128,4,8,128]{4,1,3,2,0:T(8,128)(2,1)} %copy.56), calls=%async_computation.5 | async-start | bytes 4194304 | tf_op jit(solution)/shard_map/all_to_all | solution.py:41
  91.3 0.9 fusion.1
  92.5 1.2 all-to-all-done.5
  93.8 3.8 %all_to_all.42 = bf16[2,256,128]{2,1,0:T(8,128)(2,1)S(1)} all-to-all(bf16[2,256,128]{2,1,0:T(8,128)(2,1)S(1)} %broadcast_in_dim.48), channel_id=1, replica_groups=mesh['seq'=4,'x'=4,'z'=8,'core'=2] {'core'}, dimensions={0} | all-to-all | bytes 262144 | tf_op jit(solution)/shard_map/all_to_all | solution.py:46
  97.6 0.7 fusion
  98.3 29.4 %all_to_all.43 = bf16[4,8,128,256]{2,3,1,0:T(8,128)(2,1)S(1)} all-to-all(bf16[4,8,128,256]{2,3,1,0:T(8,128)(2,1)S(1)} %fusion), channel_id=1, replica_groups=mesh['seq'=4,'x'=4,'z'=8,'core'=2] {'x'}, dimensions={0} | all-to-all | bytes 4194304 | tf_op jit(solution)/shard_map/all_to_all | solution.py:32
  128.1 19.6 %all_to_all.44 = bf16[8,128,256]{1,2,0:T(8,128)(2,1)S(1)} all-to-all(bf16[8,128,256]{1,2,0:T(8,128)(2,1)S(1)} %reduce_sum.44), channel_id=1, replica_groups=mesh['seq'=4,'x'=4,'z'=8,'core'=2] {'z'}, dimensions={0} | all-to-all | bytes 1048576 | tf_op jit(solution)/shard_map/all_to_all | solution.py:32
  147.8 0.7 reduce_sum.45
  (49 shorter events, 3.7 us)
Async XLA Ops:
  0.9 31.7 %copy-start.2 = (f32[16,8]{0,1:T(8,128)S(1)}, f32[16,8]{0,1:T(8,128)}, u32[]{:S(2)}) copy-start(f32[16,8]{0,1:T(8,128)} %param.9) | copy-start | bytes 1540
  28.3 29.0 %all-to-all-start.1 = ((bf16[4,8,256,128]{2,3,1,0:T(8,128)(2,1)}), bf16[4,8,256,128]{2,3,1,0:T(8,128)(2,1)S(1)}, u32[]{:S(2)}, u32[]{:S(2)}) async-start(bf16[4,8,256,128]{2,3,1,0:T(8,128)(2,1)} %broadcast_in_dim.35), calls=%async_computation.1 | async-start | bytes 4194304 | tf_op jit(solution)/shard_map/all_to_all | solution.py:22
  32.7 8.9 %copy-start = (f32[16,8]{0,1:T(8,128)S(1)}, f32[16,8]{0,1:T(8,128)}, u32[]{:S(2)}) copy-start(f32[16,8]{0,1:T(8,128)} %param.10) | copy-start | bytes 1540
  32.7 9.0 %copy-start.1 = (f32[3,3,128]{2,1,0:T(4,128)S(1)}, f32[3,3,128]{2,1,0:T(4,128)}, u32[]{:S(2)}) copy-start(f32[3,3,128]{2,1,0:T(4,128)} %param.8) | copy-start | bytes 13828
  58.0 7.9 %slice-start = ((s8[6291456]{0:T(1024)(128)(4,1)}), s8[4194304]{0:T(1024)(128)(4,1)S(1)}, s32[]{:S(2)}) async-start(s8[6291456]{0:T(1024)(128)(4,1)} %bitcast.77), calls=%async_computation.8 | async-start | bytes 8388608
  65.4 1.6 %slice-start.1 = ((s8[6291456]{0:T(1024)(128)(4,1)}), s8[2097152]{0:T(1024)(128)(4,1)S(1)}, s32[]{:S(2)}) async-start(s8[6291456]{0:T(1024)(128)(4,1)} %bitcast.77), calls=%async_computation.9 | async-start | bytes 4194304
  69.4 5.5 %collective-permute-start = (bf16[2,384]{1,0:T(2,128)(2,1)S(1)}, bf16[2,384]{1,0:T(2,128)(2,1)S(1)}, u32[]{:S(2)}, u32[]{:S(2)}) collective-permute-start(bf16[2,384]{1,0:T(2,128)(2,1)S(1)} %slice.51), channel_id=1, source_target_pairs={{0,64},{64,128},{128,192},{1,65},{65,129},{129,193},{2,66},{66,130... | collective-permute-start | bytes 4616 | tf_op jit(solution)/shard_map/ppermute | solution.py:14
  76.3 10.8 %all-to-all-start.3 = ((f32[4,16,128]{2,1,0:T(8,128)}), f32[4,16,128]{2,1,0:T(8,128)S(1)}, u32[]{:S(2)}, u32[]{:S(2)}) async-start(f32[4,16,128]{2,1,0:T(8,128)} %broadcast_in_dim.47), calls=%async_computation.3 | async-start | bytes 65536 | tf_op jit(solution)/shard_map/all_to_all | solution.py:22
  87.1 6.6 %all-to-all-start.5 = ((bf16[2,128,4,8,128]{4,1,3,2,0:T(8,128)(2,1)}), bf16[2,128,4,8,128]{4,1,3,2,0:T(8,128)(2,1)S(1)}, u32[]{:S(2)}, u32[]{:S(2)}) async-start(bf16[2,128,4,8,128]{4,1,3,2,0:T(8,128)(2,1)} %copy.56), calls=%async_computation.5 | async-start | bytes 4194304 | tf_op jit(solution)/shard_map/all_to_all | solution.py:41

commit v6 on v5

--- a/solution.py
+++ b/solution.py
@@ -24,7 +24,8 @@
 
 def gather_features(tokens):
     rows = tokens.shape[0]
-    every = spread_to(spread_to(spread_to(tokens, "z"), "x"), "core")
+    along_z = spread_to(tokens, "z")
+    every = spread_to(spread_to(along_z, "x"), "core")
     return every.transpose(3, 1, 2, 0, 4).reshape(rows, -1)
 
 
@@ -37,21 +38,19 @@
     rows, model_width = out_weight.shape
     nx, nz = lax.axis_size("x"), lax.axis_size("z")
     width = model_width // (nx * nz * 2)
-    split = out_weight.reshape(rows, nx, nz, 2, width).transpose(3, 0, 1, 2, 4)
-    return lax.all_to_all(split, "core", 0, 0, tiled=True)
+    split = out_weight.reshape(rows, nx, nz, 2, width).transpose(1, 3, 0, 2, 4)
+    return lax.all_to_all(split.reshape(nx * 2, rows, nz, width), ("x", "core"), 0, 0, tiled=True)
 
 
 def project_out(weight_pair, gated_out):
-    both = jnp.broadcast_to(gated_out[None], (2,) + gated_out.shape)
-    inputs_pair = lax.all_to_all(both, "core", 0, 0, tiled=True)
+    inputs_pair = spread_to(gated_out, ("x", "core"))
     return jnp.einsum(
-        "crxzw,ctr->xzwt", weight_pair, inputs_pair, preferred_element_type=jnp.float32
+        "krzw,ktr->zwt", weight_pair, inputs_pair, preferred_element_type=jnp.float32
     )
 
 
 def sum_over_channels(partial):
-    by_x = summed_over(partial, "x")
-    return summed_over(by_x, "z")
+    return summed_over(partial, "z")
 
 
 def from_earlier_blocks(end_state, block_rates, group_width):
@@ -157,6 +156,4 @@
         P(CH, None),
     )
     out_specs = P("seq", CH)
-    return jax.shard_map(
-        on_device, mesh=fine_mesh(mesh), in_specs=in_specs, out_specs=out_specs, check_vma=False
-    )
+    return jax.shard_map(on_device, mesh=fine_mesh(mesh), in_specs=in_specs, out_specs=out_specs, check_vma=False)

time: 150 us -> 153 us (1.020)
  waiting for transfers between devices: 18.9 us -> 43 us
  blocking collectives: 86 us -> 65.7 us
    all_to_all x2 -> x1, blocking collectives: 49 us -> 19.8 us  [summed_over(): got = lax.all_to_all(parts.astype(jnp.bfloat16), axis, 0, 0, tiled=True)]
    all_to_all x1, waiting for transfers between devices: 1.25 us -> 22.9 us  [pair_rows(): lax.all_to_all(split.reshape(nx * 2, rows, nz, width), ('x', 'core'), 0,...]
    all_to_all x2 -> x3, blocking collectives: 33.1 us -> 45.9 us  [spread_to(): lax.all_to_all(jnp.broadcast_to(block[None], (count,) + block.shape), axi...]
    reshape x0 -> x2, local copies, waits for them, and re-layouts: none -> 5.93 us  [pair_rows(): split = out_weight.reshape(rows, nx, nz, 2, width).transpose(1, 3, 0, 2, 4)]
    all_to_all x1 -> x0, blocking collectives: 3.84 us -> none  [project_out(): inputs_pair = lax.all_to_all(both, 'core', 0, 0, tiled=True)]
    unnamed x15 -> x14, local copies, waits for them, and re-layouts: 14.1 us -> 10.7 us
    transpose x1 -> x0, local copies, waits for them, and re-layouts: 2.63 us -> none  [pair_rows(): split = out_weight.reshape(rows, nx, nz, 2, width).transpose(3, 0, 1, 2, 4)]
    all_to_all x2, waiting for transfers between devices: 13.5 us -> 16 us  [spread_to(): lax.all_to_all(jnp.broadcast_to(block[None], (count,) + block.shape), axi...]
  transfers between devices with their start and end apart: 4 -> 4, of which waited for: 3 -> 3; matrix products, arithmetic and copies ran while one was open for 13% -> 12% of each run, Pallas kernels for 0% -> 0%
where the time goes in v6:
time: 153 us; the launch traced here: 152 us
  blocking collectives  65.7 us (43%)
  waiting for transfers between devices  43 us (28%)
  local copies, waits for them, and re-layouts  21.1 us (14%)
  starting transfers between devices  13.9 us (9%)
  matrix products  4.66 us (3%)
  other arithmetic  3.13 us (2%)
    all_to_all x3, blocking collectives, spread_to(): lax.all_to_all(jnp.broadcast_to(block[None], (count,) + block.shape), axi...  45.9 us
    all_to_all x1, waiting for transfers between devices, pair_rows(): lax.all_to_all(split.reshape(nx * 2, rows, nz, width), ('x', 'core'), 0,...  22.9 us
    all_to_all x1, blocking collectives, summed_over(): got = lax.all_to_all(parts.astype(jnp.bfloat16), axis, 0, 0, tiled=True)  19.8 us
    all_to_all x2, waiting for transfers between devices, spread_to(): lax.all_to_all(jnp.broadcast_to(block[None], (count,) + block.shape), axi...  16 us
    unnamed x14, local copies, waits for them, and re-layouts  10.7 us
    all_to_all x2, starting transfers between devices, spread_to(): lax.all_to_all(jnp.broadcast_to(block[None], (count,) + block.shape), axi...  8.98 us
    reshape x2, local copies, waits for them, and re-layouts, pair_rows(): split = out_weight.reshape(rows, nx, nz, 2, width).transpose(1, 3, 0, 2, 4)  5.93 us
    ppermute x1, waiting for transfers between devices, passed_along(): return lax.ppermute(block, axis, route)  4.16 us
  transfers between devices with their start and end apart: 4, of which 3 were waited for; matrix products, arithmetic and copies ran while one was open for 12% of the time, Pallas kernels for 0%

profile of v6, /device:TPU:24, one launch (start us, length us, event | category | flops | bytes accessed | tf_op | source)
XLA Modules:
  0.0 151.8 jit_solution(13697423366148391741)
XLA Ops:
  0.0 0.9 copy.41
  1.0 25.8 %all_to_all.35 = bf16[8,256,128]{1,2,0:T(8,128)(2,1)S(1)} all-to-all(bf16[8,256,128]{1,2,0:T(8,128)(2,1)S(1)} %broadcast_in_dim.34), channel_id=1, replica_groups=mesh['seq'=4,'x'=4,'z'=8,'core'=2] {'z'}, dimensions={0} | all-to-all | bytes 1048576 | tf_op jit(solution)/shard_map/all_to_all | solution.py:22
  26.7 1.6 %broadcast_in_dim.35 = bf16[4,8,256,128]{2,3,1,0:T(8,128)(2,1)} broadcast(bf16[8,256,128]{1,2,0:T(8,128)(2,1)S(1)} %all_to_all.35), dimensions={1,2,3} | broadcast | bytes 2621440 | tf_op jit(solution)/shard_map/broadcast_in_dim | solution.py:22
  28.3 4.3 %all-to-all-start.1 = ((bf16[4,8,256,128]{2,3,1,0:T(8,128)(2,1)}), bf16[4,8,256,128]{2,3,1,0:T(8,128)(2,1)S(1)}, u32[]{:S(2)}, u32[]{:S(2)}) async-start(bf16[4,8,256,128]{2,3,1,0:T(8,128)(2,1)} %broadcast_in_dim.35), calls=%async_computation.1 | async-start | bytes 4194304 | tf_op jit(solution)/shard_map/all_to_all | solution.py:22
  32.6 8.6 %copy.43 = bf16[8192,3,128]{0,2,1:T(8,128)(2,1)} copy(bf16[8192,3,128]{2,0,1:T(8,128)(2,1)} %param.7) | data formatting | bytes 12582912 | tf_op args[1]
  41.3 16.0 %all-to-all-done.1 = bf16[4,8,256,128]{2,3,1,0:T(8,128)(2,1)S(1)} async-done(((bf16[4,8,256,128]{2,3,1,0:T(8,128)(2,1)}), bf16[4,8,256,128]{2,3,1,0:T(8,128)(2,1)S(1)}, u32[]{:S(2)}, u32[]{:S(2)}) %all-to-all-start.1) | async-done | bytes 2097184 | tf_op jit(solution)/shard_map/all_to_all | solution.py:22
  57.3 0.7 broadcast_in_dim.36
  58.0 7.4 %all_to_all.36 = bf16[2,4,8,256,128]{3,4,2,1,0:T(8,128)(2,1)S(1)} all-to-all(bf16[2,4,8,256,128]{3,4,2,1,0:T(8,128)(2,1)S(1)} %broadcast_in_dim.36), channel_id=1, replica_groups=mesh['seq'=4,'x'=4,'z'=8,'core'=2] {'core'}, dimensions={0} | all-to-all | bytes 8388608 | tf_op jit(solution)/shard_map/all_to_all | solution.py:22
  65.9 1.1 slice-done.1
  67.0 2.4 %convolution_convert_fusion = bf16[256,384]{1,0:T(8,128)(2,1)S(1)} fusion(bf16[256,8192]{0,1:T(8,128)(2,1)S(1)} %bitcast.79, bf16[8192,384]{0,1:T(8,128)(2,1)S(1)} %bitcast.78), kind=kOutput, calls=%fused_computation.4 | convolution fusion | flops 1610711040 | bytes 10682368 | tf_op jit(solution)/shard_map/dot_general | solution.py:81
  69.4 1.3 collective-permute-start
  70.7 4.2 %collective-permute-done = bf16[2,384]{1,0:T(2,128)(2,1)S(1)} collective-permute-done((bf16[2,384]{1,0:T(2,128)(2,1)S(1)}, bf16[2,384]{1,0:T(2,128)(2,1)S(1)}, u32[]{:S(2)}, u32[]{:S(2)}) %collective-permute-start) | collective-permute-done | bytes 1568 | tf_op jit(solution)/shard_map/ppermute | solution.py:14
  75.6 0.6 broadcast_in_dim.47
  76.3 4.7 %all-to-all-start.3 = ((f32[4,16,128]{2,1,0:T(8,128)}), f32[4,16,128]{2,1,0:T(8,128)S(1)}, u32[]{:S(2)}, u32[]{:S(2)}) async-start(f32[4,16,128]{2,1,0:T(8,128)} %broadcast_in_dim.47), calls=%async_computation.3 | async-start | bytes 65536 | tf_op jit(solution)/shard_map/all_to_all | solution.py:22
  81.0 3.2 %reshape.123 = bf16[128,4,8,2,128]{4,3,2,1,0:T(2,128)(2,1)S(1)} reshape(bf16[128,8192]{1,0:T(8,128)(2,1)} %param.11) | data formatting | bytes 4194304 | tf_op jit(solution)/shard_map/reshape | solution.py:41
  84.3 2.7 %copy.54 = bf16[128,4,8,2,128]{4,0,2,3,1:T(8,128)(2,1)} copy(bf16[128,4,8,2,128]{4,3,2,1,0:T(2,128)(2,1)S(1)} %reshape.123) | data formatting | bytes 4194304 | tf_op jit(solution)/shard_map/reshape | solution.py:41
  87.0 3.6 %all-to-all-start.5 = ((bf16[8,128,8,128]{3,1,2,0:T(8,128)(2,1)}), bf16[8,128,8,128]{3,1,2,0:T(8,128)(2,1)S(1)}, u32[]{:S(2)}, u32[]{:S(2)}) async-start(bf16[8,128,8,128]{3,1,2,0:T(8,128)(2,1)} %bitcast.21), calls=%async_computation.5 | async-start | bytes 4194304 | tf_op jit(solution)/shard_map/all_to_all | solution.py:42
  91.3 2.0 %multiply_reduce_fusion = f32[8,128,128]{2,1,0:T(8,128)S(1)} fusion(f32[128,128]{1,0:T(8,128)S(1)} %maximum_convert_fusion.1, f32[16,8]{1,0:T(8,128)S(1)} %copy.46, f32[16,8]{1,0:T(8,128)S(1)} %copy.45), kind=kLoop, calls=%fused_computation | loop fusion | flops 6160384 | bytes 590848 | tf_op jit(solution)/shard_map/reduce_sum | solution.py:104
  93.7 0.9 fusion.2
  94.8 22.9 %all-to-all-done.5 = bf16[8,128,8,128]{3,1,2,0:T(8,128)(2,1)S(1)} async-done(((bf16[8,128,8,128]{3,1,2,0:T(8,128)(2,1)}), bf16[8,128,8,128]{3,1,2,0:T(8,128)(2,1)S(1)}, u32[]{:S(2)}, u32[]{:S(2)}) %all-to-all-start.5) | async-done | bytes 2097184 | tf_op jit(solution)/shard_map/all_to_all | solution.py:42
  117.8 12.8 %all_to_all.37 = bf16[8,256,128]{2,1,0:T(8,128)(2,1)S(1)} all-to-all(bf16[8,256,128]{2,1,0:T(8,128)(2,1)S(1)} %broadcast_in_dim.48), channel_id=1, replica_groups=mesh['seq'=4,'x'=4,'z'=8,'core'=2] {'x','core'}, dimensions={0} | all-to-all | bytes 1048576 | tf_op jit(solution)/shard_map/all_to_all | solution.py:22
  130.5 0.7 fusion.1
  131.3 19.8 %all_to_all.38 = bf16[8,128,256]{1,2,0:T(8,128)(2,1)S(1)} all-to-all(bf16[8,128,256]{1,2,0:T(8,128)(2,1)S(1)} %fusion.1), channel_id=1, replica_groups=mesh['seq'=4,'x'=4,'z'=8,'core'=2] {'z'}, dimensions={0} | all-to-all | bytes 1048576 | tf_op jit(solution)/shard_map/all_to_all | solution.py:33
  151.1 0.7 reduce_sum.32
  (47 shorter events, 2.7 us)
Async XLA Ops:
  28.3 29.0 %all-to-all-start.1 = ((bf16[4,8,256,128]{2,3,1,0:T(8,128)(2,1)}), bf16[4,8,256,128]{2,3,1,0:T(8,128)(2,1)S(1)}, u32[]{:S(2)}, u32[]{:S(2)}) async-start(bf16[4,8,256,128]{2,3,1,0:T(8,128)(2,1)} %broadcast_in_dim.35), calls=%async_computation.1 | async-start | bytes 4194304 | tf_op jit(solution)/shard_map/all_to_all | solution.py:22
  32.6 8.6 %copy-start.1 = (f32[3,3,128]{2,1,0:T(4,128)S(1)}, f32[3,3,128]{2,1,0:T(4,128)}, u32[]{:S(2)}) copy-start(f32[3,3,128]{2,1,0:T(4,128)} %param.8) | copy-start | bytes 13828
  32.6 8.6 %copy-start.2 = (f32[16,8]{0,1:T(8,128)S(1)}, f32[16,8]{0,1:T(8,128)}, u32[]{:S(2)}) copy-start(f32[16,8]{0,1:T(8,128)} %param.9) | copy-start | bytes 1540
  58.0 7.9 %slice-start = ((s8[6291456]{0:T(1024)(128)(4,1)}), s8[4194304]{0:T(1024)(128)(4,1)S(1)}, s32[]{:S(2)}) async-start(s8[6291456]{0:T(1024)(128)(4,1)} %bitcast.76), calls=%async_computation.7 | async-start | bytes 8388608
  65.4 1.6 %slice-start.1 = ((s8[6291456]{0:T(1024)(128)(4,1)}), s8[2097152]{0:T(1024)(128)(4,1)S(1)}, s32[]{:S(2)}) async-start(s8[6291456]{0:T(1024)(128)(4,1)} %bitcast.76), calls=%async_computation.8 | async-start | bytes 4194304
  69.4 5.5 %collective-permute-start = (bf16[2,384]{1,0:T(2,128)(2,1)S(1)}, bf16[2,384]{1,0:T(2,128)(2,1)S(1)}, u32[]{:S(2)}, u32[]{:S(2)}) collective-permute-start(bf16[2,384]{1,0:T(2,128)(2,1)S(1)} %slice.51), channel_id=1, source_target_pairs={{0,64},{64,128},{128,192},{1,65},{65,129},{129,193},{2,66},{66,130... | collective-permute-start | bytes 4616 | tf_op jit(solution)/shard_map/ppermute | solution.py:14
  76.3 10.7 %all-to-all-start.3 = ((f32[4,16,128]{2,1,0:T(8,128)}), f32[4,16,128]{2,1,0:T(8,128)S(1)}, u32[]{:S(2)}, u32[]{:S(2)}) async-start(f32[4,16,128]{2,1,0:T(8,128)} %broadcast_in_dim.47), calls=%async_computation.3 | async-start | bytes 65536 | tf_op jit(solution)/shard_map/all_to_all | solution.py:22
  84.3 6.8 %copy-start = (f32[16,8]{0,1:T(8,128)S(1)}, f32[16,8]{0,1:T(8,128)}, u32[]{:S(2)}) copy-start(f32[16,8]{0,1:T(8,128)} %param.10) | copy-start | bytes 1540
  87.0 30.7 %all-to-all-start.5 = ((bf16[8,128,8,128]{3,1,2,0:T(8,128)(2,1)}), bf16[8,128,8,128]{3,1,2,0:T(8,128)(2,1)S(1)}, u32[]{:S(2)}, u32[]{:S(2)}) async-start(bf16[8,128,8,128]{3,1,2,0:T(8,128)(2,1)} %bitcast.21), calls=%async_computation.5 | async-start | bytes 4194304 | tf_op jit(solution)/shard_map/all_to_all | solution.py:42

commit v7 on v5

--- a/solution.py
+++ b/solution.py
@@ -33,17 +33,16 @@
     return jnp.sum(got.astype(jnp.float32), axis=0)
 
 
-def pair_rows(out_weight):
+def project_out(out_weight, gated_out):
     rows, model_width = out_weight.shape
     nx, nz = lax.axis_size("x"), lax.axis_size("z")
     width = model_width // (nx * nz * 2)
     split = out_weight.reshape(rows, nx, nz, 2, width).transpose(3, 0, 1, 2, 4)
-    return lax.all_to_all(split, "core", 0, 0, tiled=True)
-
-
-def project_out(weight_pair, gated_out):
     both = jnp.broadcast_to(gated_out[None], (2,) + gated_out.shape)
-    inputs_pair = lax.all_to_all(both, "core", 0, 0, tiled=True)
+    sent = jnp.concatenate([split.reshape(2, -1), both.reshape(2, -1)], axis=1)
+    got = lax.all_to_all(sent, "core", 0, 0, tiled=True)
+    weight_pair = got[:, : split[0].size].reshape(split.shape)
+    inputs_pair = got[:, split[0].size :].reshape(both.shape)
     return jnp.einsum(
         "crxzw,ctr->xzwt", weight_pair, inputs_pair, preferred_element_type=jnp.float32
     )
@@ -77,7 +76,6 @@
     group_width = width_here // filter_count
     tokens_all = rows_here * lax.axis_size("seq")
     flat_weight = in_weight.reshape(model_width, 3 * width_here)
-    out_weight_pair = pair_rows(out_weight)
     gathered = gather_features(tokens)
     projected = jnp.dot(gathered, flat_weight, preferred_element_type=jnp.float32).astype(
         jnp.bfloat16
@@ -134,7 +132,7 @@
     )
     convolved = (local_part + carried).reshape(rows_here, width_here)
     gated_out = (query_stream * convolved).astype(jnp.bfloat16)
-    turned = sum_over_channels(project_out(out_weight_pair, gated_out))
+    turned = sum_over_channels(project_out(out_weight, gated_out))
     mixed = turned.T.astype(jnp.bfloat16)
     return mixed
 

time: 150 us -> 201 us (1.34)
  other arithmetic: 3.51 us -> 40.6 us
  local copies, waits for them, and re-layouts: 21 us -> 35.9 us
  starting transfers between devices: 14 us -> 10.4 us
  blocking collectives: 86 us -> 88.5 us
    all_to_all x0 -> x2, other arithmetic: none -> 36.6 us  [project_out(): got = lax.all_to_all(sent, 'core', 0, 0, tiled=True)]
    unnamed x15 -> x24, local copies, waits for them, and re-layouts: 14.1 us -> 27.5 us
    all_to_all x1 -> x0, starting transfers between devices: 3.76 us -> none  [pair_rows(): return lax.all_to_all(split, 'core', 0, 0, tiled=True)]
    reshape x0 -> x1, local copies, waits for them, and re-layouts: none -> 2.71 us  [project_out(): split = out_weight.reshape(rows, nx, nz, 2, width).transpose(3, 0, 1, 2, 4)]
    transpose x1 -> x0, local copies, waits for them, and re-layouts: 2.63 us -> none  [pair_rows(): split = out_weight.reshape(rows, nx, nz, 2, width).transpose(3, 0, 1, 2, 4)]
    all_to_all x1, blocking collectives: 3.84 us -> 6.43 us  [project_out(): got = lax.all_to_all(sent, 'core', 0, 0, tiled=True)]
  transfers between devices with their start and end apart: 4 -> 3, of which waited for: 3 -> 2; matrix products, arithmetic and copies ran while one was open for 13% -> 8% of each run, Pallas kernels for 0% -> 0%
where the time goes in v7:
time: 201 us; the launch traced here: 199 us
  blocking collectives  88.5 us (44%)
  other arithmetic  40.6 us (20%)
  local copies, waits for them, and re-layouts  35.9 us (18%)
  waiting for transfers between devices  17 us (8%)
  starting transfers between devices  10.4 us (5%)
  matrix products  6.33 us (3%)
    all_to_all x2, blocking collectives, summed_over(): got = lax.all_to_all(parts.astype(jnp.bfloat16), axis, 0, 0, tiled=True)  49 us
    all_to_all x2, other arithmetic, project_out(): got = lax.all_to_all(sent, 'core', 0, 0, tiled=True)  36.6 us
    all_to_all x2, blocking collectives, spread_to(): lax.all_to_all(jnp.broadcast_to(block[None], (count,) + block.shape), axi...  33.1 us
    unnamed x24, local copies, waits for them, and re-layouts  27.5 us
    all_to_all x2, waiting for transfers between devices, spread_to(): lax.all_to_all(jnp.broadcast_to(block[None], (count,) + block.shape), axi...  12.9 us
    all_to_all x2, starting transfers between devices, spread_to(): lax.all_to_all(jnp.broadcast_to(block[None], (count,) + block.shape), axi...  9.11 us
    all_to_all x1, blocking collectives, project_out(): got = lax.all_to_all(sent, 'core', 0, 0, tiled=True)  6.43 us
    ppermute x1, waiting for transfers between devices, passed_along(): return lax.ppermute(block, axis, route)  4.15 us
  transfers between devices with their start and end apart: 3, of which 2 were waited for; matrix products, arithmetic and copies ran while one was open for 8% of the time, Pallas kernels for 0%

profile of v7, /device:TPU:24, one launch (start us, length us, event | category | flops | bytes accessed | tf_op | source)
XLA Modules:
  0.0 199.1 jit_solution(7141929076644711005)
XLA Ops:
  1.0 25.8 %all_to_all.42 = bf16[8,256,128]{1,2,0:T(8,128)(2,1)S(1)} all-to-all(bf16[8,256,128]{1,2,0:T(8,128)(2,1)S(1)} %broadcast_in_dim.36), channel_id=1, replica_groups=mesh['seq'=4,'x'=4,'z'=8,'core'=2] {'z'}, dimensions={0} | all-to-all | bytes 1048576 | tf_op jit(solution)/shard_map/all_to_all | solution.py:22
  26.7 1.6 broadcast_in_dim.37
  28.3 4.4 %all-to-all-start.1 = ((bf16[4,8,256,128]{2,3,1,0:T(8,128)(2,1)}), bf16[4,8,256,128]{2,3,1,0:T(8,128)(2,1)S(1)}, u32[]{:S(2)}, u32[]{:S(2)}) async-start(bf16[4,8,256,128]{2,3,1,0:T(8,128)(2,1)} %broadcast_in_dim.37), calls=%async_computation.1 | async-start | bytes 4194304 | tf_op jit(solution)/shard_map/all_to_all | solution.py:22
  32.8 8.7 %copy.56 = bf16[8192,3,128]{0,2,1:T(8,128)(2,1)} copy(bf16[8192,3,128]{2,0,1:T(8,128)(2,1)} %param.7) | data formatting | bytes 12582912 | tf_op args[1]
  42.6 2.0 multiply_reduce_fusion
  44.6 12.9 %all-to-all-done.1 = bf16[4,8,256,128]{2,3,1,0:T(8,128)(2,1)S(1)} async-done(((bf16[4,8,256,128]{2,3,1,0:T(8,128)(2,1)}), bf16[4,8,256,128]{2,3,1,0:T(8,128)(2,1)S(1)}, u32[]{:S(2)}, u32[]{:S(2)}) %all-to-all-start.1) | async-done | bytes 2097184 | tf_op jit(solution)/shard_map/all_to_all | solution.py:22
  58.1 7.4 %all_to_all.43 = bf16[2,4,8,256,128]{3,4,2,1,0:T(8,128)(2,1)S(1)} all-to-all(bf16[2,4,8,256,128]{3,4,2,1,0:T(8,128)(2,1)S(1)} %broadcast_in_dim.38), channel_id=1, replica_groups=mesh['seq'=4,'x'=4,'z'=8,'core'=2] {'core'}, dimensions={0} | all-to-all | bytes 8388608 | tf_op jit(solution)/shard_map/all_to_all | solution.py:22
  66.0 1.1 slice-done.1
  67.1 2.4 %convolution_convert_fusion = bf16[256,384]{1,0:T(8,128)(2,1)S(1)} fusion(bf16[256,8192]{0,1:T(8,128)(2,1)S(1)} %bitcast.90, bf16[8192,384]{0,1:T(8,128)(2,1)S(1)} %bitcast.89), kind=kOutput, calls=%fused_computation.6 | convolution fusion | flops 1610711040 | bytes 10682368 | tf_op jit(solution)/shard_map/dot_general | solution.py:80
  69.5 1.3 collective-permute-start
  70.8 4.1 %collective-permute-done = bf16[2,384]{1,0:T(2,128)(2,1)S(1)} collective-permute-done((bf16[2,384]{1,0:T(2,128)(2,1)S(1)}, bf16[2,384]{1,0:T(2,128)(2,1)S(1)}, u32[]{:S(2)}, u32[]{:S(2)}) %collective-permute-start) | collective-permute-done | bytes 1568 | tf_op jit(solution)/shard_map/ppermute | solution.py:14
  76.4 4.7 %all-to-all-start.3 = ((f32[4,16,128]{2,1,0:T(8,128)}), f32[4,16,128]{2,1,0:T(8,128)S(1)}, u32[]{:S(2)}, u32[]{:S(2)}) async-start(f32[4,16,128]{2,1,0:T(8,128)} %broadcast_in_dim.49), calls=%async_computation.3 | async-start | bytes 65536 | tf_op jit(solution)/shard_map/all_to_all | solution.py:22
  81.9 2.7 %reshape.129 = bf16[128,4,8,2,128]{4,3,2,1,0:T(2,128)(2,1)} reshape(bf16[128,8192]{1,0:T(8,128)(2,1)S(1)} %copy-done) | data formatting | bytes 4194304 | tf_op jit(solution)/shard_map/reshape | solution.py:40
  85.0 1.6 fusion.1
  87.0 14.4 %maximum_bitcast_fusion = bf16[2,1,557056]{2,0,1:T(2,128)(2,1)S(1)} fusion(bf16[2,524288]{1,0:T(2,128)(2,1)} %bitcast.86, bf16[557056]{0:T(1024)(128)(2,1)S(1)} %pad.2.clone), kind=kLoop, calls=%fused_computation.2 | loop fusion | flops 4456448 | bytes 5439488 | tf_op jit(solution)/shard_map/all_to_all | solution.py:43
  102.0 22.1 %reduce.2 = bf16[2,557056]{1,0:T(2,128)(2,1)} reduce(bf16[2,1,557056]{2,0,1:T(2,128)(2,1)S(1)} %maximum_bitcast_fusion, bf16[]{:T(256)} %broadcast.89), dimensions={1}, to_apply=%copy.67.reduce_sub_computation | reduce | bytes 4456450 | tf_op jit(solution)/shard_map/all_to_all | solution.py:43
  124.1 3.3 %reshape.145 = bf16[2,2,278528]{2,1,0:T(2,128)(2,1)S(1)} reshape(bf16[2,557056]{1,0:T(2,128)(2,1)} %reduce.2) | data formatting | bytes 4456448
  127.4 6.4 %all_to_all.44 = bf16[2,2,278528]{2,1,0:T(2,128)(2,1)} all-to-all(bf16[2,2,278528]{2,1,0:T(2,128)(2,1)S(1)} %reshape.145), channel_id=1, replica_groups=mesh['seq'=4,'x'=4,'z'=8,'core'=2] {'core'}, dimensions={0} | all-to-all | bytes 4456448 | tf_op jit(solution)/shard_map/all_to_all | solution.py:43
  133.8 4.5 %reshape.146 = bf16[2,1,557056]{2,1,0:T(2,128)(2,1)} reshape(bf16[2,2,278528]{2,1,0:T(2,128)(2,1)} %all_to_all.44) | data formatting | bytes 4456448
  138.3 7.0 %copy.92 = bf16[2,1,557056]{2,0,1:T(2,128)(2,1)S(1)} copy(bf16[2,1,557056]{2,1,0:T(2,128)(2,1)} %reshape.146) | data formatting | bytes 4456448
  145.3 1.5 slice_bitcast_fusion
  147.2 1.7 bitcast_convert_fusion
  148.9 29.4 %all_to_all.45 = bf16[4,8,128,256]{3,2,1,0:T(8,128)(2,1)S(1)} all-to-all(bf16[4,8,128,256]{3,2,1,0:T(8,128)(2,1)S(1)} %bitcast_convert_fusion), channel_id=1, replica_groups=mesh['seq'=4,'x'=4,'z'=8,'core'=2] {'x'}, dimensions={0} | all-to-all | bytes 4194304 | tf_op jit(solution)/shard_map/all_to_all | solution.py:32
  178.7 19.6 %all_to_all.46 = bf16[8,128,256]{2,1,0:T(8,128)(2,1)S(1)} all-to-all(bf16[8,128,256]{2,1,0:T(8,128)(2,1)S(1)} %reduce_sum.44), channel_id=1, replica_groups=mesh['seq'=4,'x'=4,'z'=8,'core'=2] {'z'}, dimensions={0} | all-to-all | bytes 1048576 | tf_op jit(solution)/shard_map/all_to_all | solution.py:32
  (60 shorter events, 8.1 us)
Async XLA Ops:
  28.3 4.4 %copy-start.3 = (f32[16,8]{0,1:T(8,128)S(1)}, f32[16,8]{0,1:T(8,128)}, u32[]{:S(2)}) copy-start(f32[16,8]{0,1:T(8,128)} %param.9) | copy-start | bytes 1540
  28.3 29.1 %all-to-all-start.1 = ((bf16[4,8,256,128]{2,3,1,0:T(8,128)(2,1)}), bf16[4,8,256,128]{2,3,1,0:T(8,128)(2,1)S(1)}, u32[]{:S(2)}, u32[]{:S(2)}) async-start(bf16[4,8,256,128]{2,3,1,0:T(8,128)(2,1)} %broadcast_in_dim.37), calls=%async_computation.1 | async-start | bytes 4194304 | tf_op jit(solution)/shard_map/all_to_all | solution.py:22
  32.8 8.9 %copy-start.1 = (f32[16,8]{0,1:T(8,128)S(1)}, f32[16,8]{0,1:T(8,128)}, u32[]{:S(2)}) copy-start(f32[16,8]{0,1:T(8,128)} %param.10) | copy-start | bytes 1540
  32.8 9.6 %copy-start.2 = (f32[3,3,128]{2,1,0:T(4,128)S(1)}, f32[3,3,128]{2,1,0:T(4,128)}, u32[]{:S(2)}) copy-start(f32[3,3,128]{2,1,0:T(4,128)} %param.8) | copy-start | bytes 13828
  58.1 7.9 %slice-start = ((s8[6291456]{0:T(1024)(128)(4,1)}), s8[4194304]{0:T(1024)(128)(4,1)S(1)}, s32[]{:S(2)}) async-start(s8[6291456]{0:T(1024)(128)(4,1)} %bitcast.87), calls=%async_computation.7 | async-start | bytes 8388608
  65.5 1.6 slice-start.1
  69.5 5.5 %collective-permute-start = (bf16[2,384]{1,0:T(2,128)(2,1)S(1)}, bf16[2,384]{1,0:T(2,128)(2,1)S(1)}, u32[]{:S(2)}, u32[]{:S(2)}) collective-permute-start(bf16[2,384]{1,0:T(2,128)(2,1)S(1)} %slice.59), channel_id=1, source_target_pairs={{0,64},{64,128},{128,192},{1,65},{65,129},{129,193},{2,66},{66,130... | collective-permute-start | bytes 4616 | tf_op jit(solution)/shard_map/ppermute | solution.py:14
  70.8 11.1 %copy-start = (bf16[128,8192]{1,0:T(8,128)(2,1)S(1)}, bf16[128,8192]{1,0:T(8,128)(2,1)}, u32[]{:S(2)}) copy-start(bf16[128,8192]{1,0:T(8,128)(2,1)} %param.11) | copy-start | bytes 6291460
  76.4 8.2 %all-to-all-start.3 = ((f32[4,16,128]{2,1,0:T(8,128)}), f32[4,16,128]{2,1,0:T(8,128)S(1)}, u32[]{:S(2)}, u32[]{:S(2)}) async-start(f32[4,16,128]{2,1,0:T(8,128)} %broadcast_in_dim.49), calls=%async_computation.3 | async-start | bytes 65536 | tf_op jit(solution)/shard_map/all_to_all | solution.py:22
  81.9 2.8 %copy-start.4 = (f32[128]{0:T(128)S(1)}, f32[128]{0:T(128)}, u32[]{:S(2)}) copy-start(f32[128]{0:T(128)} %iota_add_fusion) | copy-start | bytes 1540

commit v8 on v5

--- a/solution.py
+++ b/solution.py
@@ -82,22 +82,79 @@
     projected = jnp.dot(gathered, flat_weight, preferred_element_type=jnp.float32).astype(
         jnp.bfloat16
     )
-    previous = passed_along(projected[rows_here - (TAPS - 1) :], "seq", 1)
-    padded = jnp.concatenate([previous, projected], axis=0).astype(jnp.float32)
     flat_taps = short_taps.reshape(TAPS, 3 * width_here)
-    filtered = jnp.zeros((rows_here, 3 * width_here), jnp.float32)
-    for shift_back in range(TAPS):
-        filtered = (
-            filtered
-            + flat_taps[shift_back]
-            * padded[TAPS - 1 - shift_back : TAPS - 1 - shift_back + rows_here]
-        )
-    query_stream = filtered[:, :width_here]
-    gated_in = filtered[:, width_here : 2 * width_here] * filtered[:, 2 * width_here :]
+    head = projected[: TAPS - 1].astype(jnp.float32)
+    tail = projected[rows_here - (TAPS - 1) :].astype(jnp.float32)
+
+    def gated_with(previous):
+        padded = jnp.concatenate([previous, projected.astype(jnp.float32)], axis=0)
+        filtered = jnp.zeros((rows_here, 3 * width_here), jnp.float32)
+        for shift_back in range(TAPS):
+            filtered = (
+                filtered
+                + flat_taps[shift_back]
+                * padded[TAPS - 1 - shift_back : TAPS - 1 - shift_back + rows_here]
+            )
+        return filtered[:, :width_here], filtered[:, width_here : 2 * width_here] * filtered[:, 2 * width_here :]
+
+    def head_gated(previous, first):
+        padded = jnp.concatenate([previous, first], axis=0)
+        filtered = jnp.zeros((TAPS - 1, 3 * width_here), jnp.float32)
+        for shift_back in range(TAPS):
+            filtered = filtered + flat_taps[shift_back] * padded[TAPS - 1 - shift_back : 2 * (TAPS - 1) - shift_back]
+        return filtered[:, width_here : 2 * width_here] * filtered[:, 2 * width_here :]
+
+    no_previous = jnp.zeros((TAPS - 1, 3 * width_here), jnp.float32)
+    _, gated_alone = gated_with(no_previous)
     block_len = math.gcd(rows_here, 128)
     block_count = rows_here // block_len
     scaled_rates = decay_rates / tokens_all
     offsets_in = jnp.arange(block_len, dtype=jnp.float32)
+    end_weights = jnp.exp(-scaled_rates[:, :, None] * (block_len - 1 - offsets_in)[None, None, :])
+    inner_decay = jnp.exp(-scaled_rates * block_len)[:, :, None]
+
+    def ends_of(gated):
+        blocks = gated.reshape(block_count, block_len, filter_count, group_width)
+        ends = jnp.einsum("mgs,bsgi->bmgi", end_weights, blocks, precision=lax.Precision.HIGHEST)
+        running = jnp.zeros((mode_count, filter_count, group_width), jnp.float32)
+        starts_list = []
+        for block_number in range(block_count):
+            starts_list.append(running)
+            running = inner_decay * running + ends[block_number]
+        return jnp.stack(starts_list, axis=0), running.reshape(mode_count, width_here)
+
+    _, end_alone = ends_of(gated_alone)
+    packed = jnp.concatenate(
+        [end_alone, head.reshape(-1, width_here), tail.reshape(-1, width_here)], axis=0
+    )
+    every = spread_to(packed, "seq")
+    blocks_seq = lax.axis_size("seq")
+    here = lax.axis_index("seq")
+    source = jnp.arange(blocks_seq)
+    heads = every[:, mode_count : mode_count + 3 * (TAPS - 1)].reshape(blocks_seq, TAPS - 1, 3 * width_here)
+    tails = every[:, mode_count + 3 * (TAPS - 1) :].reshape(blocks_seq, TAPS - 1, 3 * width_here)
+    tails_before = jnp.where(
+        (source >= 1)[:, None, None], jnp.roll(tails, 1, axis=0), 0.0
+    )
+    head_decay = jnp.repeat(
+        jnp.exp(-scaled_rates[None] * (rows_here - 1 - jnp.arange(TAPS - 1, dtype=jnp.float32))[:, None, None]),
+        group_width,
+        axis=2,
+    )
+    fixes = []
+    for j in range(blocks_seq):
+        delta = head_gated(tails_before[j], heads[j]) - head_gated(no_previous, heads[j])
+        fixes.append(jnp.sum(head_decay * delta[:, None, :], axis=0))
+    end_states = every[:, :mode_count] + jnp.stack(fixes, axis=0)
+    between = jnp.maximum(here - 1 - source, 0).astype(jnp.float32)
+    decay = jnp.where(
+        (source < here)[:, None, None],
+        jnp.exp(-(scaled_rates * rows_here)[None] * between[:, None, None]),
+        0.0,
+    )
+    incoming = jnp.sum(jnp.repeat(decay, group_width, axis=2) * end_states, axis=0)
+    previous = jnp.sum(jnp.where((source == here - 1)[:, None, None], tails, 0.0), axis=0)
+    query_stream, gated_in = gated_with(previous)
     distance = jnp.arange(block_len)[:, None] - jnp.arange(block_len)[None, :]
     lag = jnp.maximum(distance, 0).astype(jnp.float32)
     toeplitz = jnp.where(
@@ -107,19 +164,7 @@
     )
     blocks_in = gated_in.reshape(block_count, block_len, filter_count, group_width)
     local_part = jnp.einsum("gts,bsgi->btgi", toeplitz, blocks_in, precision=lax.Precision.HIGHEST)
-    end_weights = jnp.exp(-scaled_rates[:, :, None] * (block_len - 1 - offsets_in)[None, None, :])
-    block_ends = jnp.einsum(
-        "mgs,bsgi->bmgi", end_weights, blocks_in, precision=lax.Precision.HIGHEST
-    )
-    inner_decay = jnp.exp(-scaled_rates * block_len)[:, :, None]
-    running = jnp.zeros((mode_count, filter_count, group_width), jnp.float32)
-    starts_list = []
-    for block_number in range(block_count):
-        starts_list.append(running)
-        running = inner_decay * running + block_ends[block_number]
-    local_starts = jnp.stack(starts_list, axis=0)
-    end_state = running.reshape(mode_count, width_here)
-    incoming = from_earlier_blocks(end_state, scaled_rates * rows_here, group_width)
+    local_starts, _ = ends_of(gated_in)
     block_offsets = (jnp.arange(block_count, dtype=jnp.float32) * block_len)[:, None, None]
     start_decay = jnp.exp(-scaled_rates[None] * block_offsets)
     block_starts = (

time: 150 us -> 148 us (0.987)
  blocking collectives: 86 us -> 60.2 us
  waiting for transfers between devices: 18.9 us -> 31.7 us
  starting transfers between devices: 14 us -> 21.2 us
  local copies, waits for them, and re-layouts: 21 us -> 23.3 us
    all_to_all x2 -> x1, blocking collectives: 33.1 us -> 7.37 us  [spread_to(): lax.all_to_all(jnp.broadcast_to(block[None], (count,) + block.shape), axi...]
    all_to_all x2 -> x3, waiting for transfers between devices: 13.5 us -> 31.7 us  [spread_to(): lax.all_to_all(jnp.broadcast_to(block[None], (count,) + block.shape), axi...]
    all_to_all x2 -> x3, starting transfers between devices: 8.98 us -> 17.4 us  [spread_to(): lax.all_to_all(jnp.broadcast_to(block[None], (count,) + block.shape), axi...]
    ppermute x1 -> x0, waiting for transfers between devices: 4.16 us -> none  [passed_along(): return lax.ppermute(block, axis, route)]
    unnamed x15 -> x13, local copies, waits for them, and re-layouts: 14.1 us -> 13.9 us
  transfers between devices with their start and end apart: 4 -> 4, of which waited for: 3 -> 2; matrix products, arithmetic and copies ran while one was open for 13% -> 15% of each run, Pallas kernels for 0% -> 0%
where the time goes in v8:
time: 148 us; the launch traced here: 147 us
  blocking collectives  60.2 us (41%)
  waiting for transfers between devices  31.7 us (21%)
  local copies, waits for them, and re-layouts  23.3 us (16%)
  starting transfers between devices  21.2 us (14%)
  matrix products  4.99 us (3%)
  other arithmetic  4.66 us (3%)
    all_to_all x2, blocking collectives, summed_over(): got = lax.all_to_all(parts.astype(jnp.bfloat16), axis, 0, 0, tiled=True)  49 us
    all_to_all x3, waiting for transfers between devices, spread_to(): lax.all_to_all(jnp.broadcast_to(block[None], (count,) + block.shape), axi...  31.7 us
    all_to_all x3, starting transfers between devices, spread_to(): lax.all_to_all(jnp.broadcast_to(block[None], (count,) + block.shape), axi...  17.4 us
    unnamed x13, local copies, waits for them, and re-layouts  13.9 us
    all_to_all x1, blocking collectives, spread_to(): lax.all_to_all(jnp.broadcast_to(block[None], (count,) + block.shape), axi...  7.37 us
    all_to_all x1, blocking collectives, project_out(): inputs_pair = lax.all_to_all(both, 'core', 0, 0, tiled=True)  3.84 us
    all_to_all x1, starting transfers between devices, pair_rows(): return lax.all_to_all(split, 'core', 0, 0, tiled=True)  3.76 us
    broadcast_in_dim x4, local copies, waits for them, and re-layouts, spread_to(): jnp.broadcast_to(block[None], (count,) + block.shape)  3.71 us
  transfers between devices with their start and end apart: 4, of which 2 were waited for; matrix products, arithmetic and copies ran while one was open for 15% of the time, Pallas kernels for 0%

profile of v8, /device:TPU:24, one launch (start us, length us, event | category | flops | bytes accessed | tf_op | source)
XLA Modules:
  0.0 146.5 jit_solution(12798160095556312885)
XLA Ops:
  0.0 0.9 copy.78
  0.9 0.8 broadcast_in_dim.56
  1.8 8.5 %all-to-all-start = ((bf16[8,256,128]{1,2,0:T(8,128)(2,1)}), bf16[8,256,128]{1,2,0:T(8,128)(2,1)S(1)}, u32[]{:S(2)}, u32[]{:S(2)}) async-start(bf16[8,256,128]{1,2,0:T(8,128)(2,1)} %broadcast_in_dim.56), calls=%async_computation | async-start | bytes 1048576 | tf_op jit(solution)/shard_map/all_to_all | solution.py:22
  10.3 0.7 multiply_negate_fusion
  11.0 16.8 %all-to-all-done = bf16[8,256,128]{1,2,0:T(8,128)(2,1)S(1)} async-done(((bf16[8,256,128]{1,2,0:T(8,128)(2,1)}), bf16[8,256,128]{1,2,0:T(8,128)(2,1)S(1)}, u32[]{:S(2)}, u32[]{:S(2)}) %all-to-all-start) | async-done | bytes 524320 | tf_op jit(solution)/shard_map/all_to_all | solution.py:22
  27.7 1.6 %broadcast_in_dim.57 = bf16[4,8,256,128]{2,3,1,0:T(8,128)(2,1)} broadcast(bf16[8,256,128]{1,2,0:T(8,128)(2,1)S(1)} %all-to-all-done), dimensions={1,2,3} | broadcast | bytes 2621440 | tf_op jit(solution)/shard_map/broadcast_in_dim | solution.py:22
  29.3 4.3 %all-to-all-start.1 = ((bf16[4,8,256,128]{2,3,1,0:T(8,128)(2,1)}), bf16[4,8,256,128]{2,3,1,0:T(8,128)(2,1)S(1)}, u32[]{:S(2)}, u32[]{:S(2)}) async-start(bf16[4,8,256,128]{2,3,1,0:T(8,128)(2,1)} %broadcast_in_dim.57), calls=%async_computation.1 | async-start | bytes 4194304 | tf_op jit(solution)/shard_map/all_to_all | solution.py:22
  33.6 8.6 %copy.80 = bf16[8192,3,128]{0,2,1:T(8,128)(2,1)} copy(bf16[8192,3,128]{2,0,1:T(8,128)(2,1)} %param.7) | data formatting | bytes 12582912 | tf_op args[1]
  43.2 2.0 %multiply_reduce_fusion = f32[8,128,128]{2,1,0:T(8,128)S(1)} fusion(f32[128,128]{1,0:T(8,128)S(1)} %maximum_convert_fusion, f32[16,8]{1,0:T(8,128)S(1)} %copy.89, f32[16,8]{1,0:T(8,128)S(1)} %copy.88), kind=kLoop, calls=%fused_computation | loop fusion | flops 6160384 | bytes 590848 | tf_op jit(solution)/shard_map/reduce_sum | solution.py:162
  45.1 15.0 %all-to-all-done.1 = bf16[4,8,256,128]{2,3,1,0:T(8,128)(2,1)S(1)} async-done(((bf16[4,8,256,128]{2,3,1,0:T(8,128)(2,1)}), bf16[4,8,256,128]{2,3,1,0:T(8,128)(2,1)S(1)}, u32[]{:S(2)}, u32[]{:S(2)}) %all-to-all-start.1) | async-done | bytes 2097184 | tf_op jit(solution)/shard_map/all_to_all | solution.py:22
  60.1 0.7 broadcast_in_dim.58
  60.8 7.4 %all_to_all.40 = bf16[2,4,8,256,128]{3,4,2,1,0:T(8,128)(2,1)S(1)} all-to-all(bf16[2,4,8,256,128]{3,4,2,1,0:T(8,128)(2,1)S(1)} %broadcast_in_dim.58), channel_id=1, replica_groups=mesh['seq'=4,'x'=4,'z'=8,'core'=2] {'core'}, dimensions={0} | all-to-all | bytes 8388608 | tf_op jit(solution)/shard_map/all_to_all | solution.py:22
  68.7 1.1 slice-done.1
  69.8 2.4 %fusion.71 = (f32[256,384]{1,0:T(8,128)S(1)}, bf16[256,384]{1,0:T(8,128)(2,1)S(1)}) fusion(bf16[256,8192]{0,1:T(8,128)(2,1)S(1)} %bitcast.86, bf16[8192,384]{0,1:T(8,128)(2,1)S(1)} %bitcast.85), kind=kOutput, calls=%fused_computation.139 | convolution fusion | flops 1610809344 | bytes 11075584 | tf_op jit(solution)/shard_map/dot_general | solution.py:82
  73.7 4.7 %all-to-all-start.3 = ((f32[4,28,128]{2,1,0:T(8,128)}), f32[4,28,128]{2,1,0:T(8,128)S(1)}, u32[]{:S(2)}, u32[]{:S(2)}) async-start(f32[4,28,128]{2,1,0:T(8,128)} %broadcast_in_dim.64), calls=%async_computation.3 | async-start | bytes 131072 | tf_op jit(solution)/shard_map/all_to_all | solution.py:22
  78.7 3.2 %copy.98 = bf16[128,8192]{0,1:T(8,128)(2,1)S(1)} copy(bf16[128,8192]{1,0:T(8,128)(2,1)} %param.11) | data formatting | bytes 4194304 | tf_op args[5]
  82.0 2.7 %copy.99 = bf16[2,128,4,8,128]{4,1,3,2,0:T(8,128)(2,1)} copy(bf16[2,128,4,8,128]{1,4,0,3,2:T(8,128)(2,1)S(1)} %bitcast.82) | data formatting | bytes 4194304 | tf_op jit(solution)/shard_map/transpose | solution.py:40
  84.6 3.8 %all-to-all-start.5 = ((bf16[2,128,4,8,128]{4,1,3,2,0:T(8,128)(2,1)}), bf16[2,128,4,8,128]{4,1,3,2,0:T(8,128)(2,1)S(1)}, u32[]{:S(2)}, u32[]{:S(2)}) async-start(bf16[2,128,4,8,128]{4,1,3,2,0:T(8,128)(2,1)} %copy.99), calls=%async_computation.5 | async-start | bytes 4194304 | tf_op jit(solution)/shard_map/all_to_all | solution.py:41
  90.7 0.9 fusion.1
  91.8 3.8 %all_to_all.41 = bf16[2,256,128]{2,1,0:T(8,128)(2,1)S(1)} all-to-all(bf16[2,256,128]{2,1,0:T(8,128)(2,1)S(1)} %broadcast_in_dim.124), channel_id=1, replica_groups=mesh['seq'=4,'x'=4,'z'=8,'core'=2] {'core'}, dimensions={0} | all-to-all | bytes 262144 | tf_op jit(solution)/shard_map/all_to_all | solution.py:46
  95.7 0.7 fusion
  96.4 29.4 %all_to_all.42 = bf16[4,8,128,256]{2,3,1,0:T(8,128)(2,1)S(1)} all-to-all(bf16[4,8,128,256]{2,3,1,0:T(8,128)(2,1)S(1)} %fusion), channel_id=1, replica_groups=mesh['seq'=4,'x'=4,'z'=8,'core'=2] {'x'}, dimensions={0} | all-to-all | bytes 4194304 | tf_op jit(solution)/shard_map/all_to_all | solution.py:32
  126.2 19.6 %all_to_all.43 = bf16[8,128,256]{1,2,0:T(8,128)(2,1)S(1)} all-to-all(bf16[8,128,256]{1,2,0:T(8,128)(2,1)S(1)} %reduce_sum.97), channel_id=1, replica_groups=mesh['seq'=4,'x'=4,'z'=8,'core'=2] {'z'}, dimensions={0} | all-to-all | bytes 1048576 | tf_op jit(solution)/shard_map/all_to_all | solution.py:32
  145.8 0.7 reduce_sum.98
  (92 shorter events, 6.0 us)
Async XLA Ops:
  1.8 26.0 %all-to-all-start = ((bf16[8,256,128]{1,2,0:T(8,128)(2,1)}), bf16[8,256,128]{1,2,0:T(8,128)(2,1)S(1)}, u32[]{:S(2)}, u32[]{:S(2)}) async-start(bf16[8,256,128]{1,2,0:T(8,128)(2,1)} %broadcast_in_dim.56), calls=%async_computation | async-start | bytes 1048576 | tf_op jit(solution)/shard_map/all_to_all | solution.py:22
  29.3 30.8 %all-to-all-start.1 = ((bf16[4,8,256,128]{2,3,1,0:T(8,128)(2,1)}), bf16[4,8,256,128]{2,3,1,0:T(8,128)(2,1)S(1)}, u32[]{:S(2)}, u32[]{:S(2)}) async-start(bf16[4,8,256,128]{2,3,1,0:T(8,128)(2,1)} %broadcast_in_dim.57), calls=%async_computation.1 | async-start | bytes 4194304 | tf_op jit(solution)/shard_map/all_to_all | solution.py:22
  33.6 9.2 %copy-start = (f32[16,8]{0,1:T(8,128)S(1)}, f32[16,8]{0,1:T(8,128)}, u32[]{:S(2)}) copy-start(f32[16,8]{0,1:T(8,128)} %param.10) | copy-start | bytes 1540
  33.6 9.4 %copy-start.1 = (f32[3,3,128]{2,1,0:T(4,128)S(1)}, f32[3,3,128]{2,1,0:T(4,128)}, u32[]{:S(2)}) copy-start(f32[3,3,128]{2,1,0:T(4,128)} %param.8) | copy-start | bytes 13828
  60.8 7.9 %slice-start = ((s8[6291456]{0:T(1024)(128)(4,1)}), s8[4194304]{0:T(1024)(128)(4,1)S(1)}, s32[]{:S(2)}) async-start(s8[6291456]{0:T(1024)(128)(4,1)} %bitcast.83), calls=%async_computation.8 | async-start | bytes 8388608
  68.2 1.6 %slice-start.1 = ((s8[6291456]{0:T(1024)(128)(4,1)}), s8[2097152]{0:T(1024)(128)(4,1)S(1)}, s32[]{:S(2)}) async-start(s8[6291456]{0:T(1024)(128)(4,1)} %bitcast.83), calls=%async_computation.9 | async-start | bytes 4194304
  73.7 10.9 %all-to-all-start.3 = ((f32[4,28,128]{2,1,0:T(8,128)}), f32[4,28,128]{2,1,0:T(8,128)S(1)}, u32[]{:S(2)}, u32[]{:S(2)}) async-start(f32[4,28,128]{2,1,0:T(8,128)} %broadcast_in_dim.64), calls=%async_computation.3 | async-start | bytes 131072 | tf_op jit(solution)/shard_map/all_to_all | solution.py:22
  84.6 7.2 %all-to-all-start.5 = ((bf16[2,128,4,8,128]{4,1,3,2,0:T(8,128)(2,1)}), bf16[2,128,4,8,128]{4,1,3,2,0:T(8,128)(2,1)S(1)}, u32[]{:S(2)}, u32[]{:S(2)}) async-start(bf16[2,128,4,8,128]{4,1,3,2,0:T(8,128)(2,1)} %copy.99), calls=%async_computation.5 | async-start | bytes 4194304 | tf_op jit(solution)/shard_map/all_to_all | solution.py:41

commit v9 on v8

--- a/solution.py
+++ b/solution.py
@@ -28,8 +28,8 @@
     return every.transpose(3, 1, 2, 0, 4).reshape(rows, -1)
 
 
-def summed_over(parts, axis):
-    got = lax.all_to_all(parts.astype(jnp.bfloat16), axis, 0, 0, tiled=True)
+def summed_over(parts, axis, wire=jnp.bfloat16):
+    got = lax.all_to_all(parts.astype(wire), axis, 0, 0, tiled=True)
     return jnp.sum(got.astype(jnp.float32), axis=0)
 
 
@@ -51,7 +51,7 @@
 
 def sum_over_channels(partial):
     by_x = summed_over(partial, "x")
-    return summed_over(by_x, "z")
+    return summed_over(by_x, "z", jnp.float32)
 
 
 def from_earlier_blocks(end_state, block_rates, group_width):

time: 148 us -> 159 us (1.074)
  blocking collectives: 60.2 us -> 71.5 us
    all_to_all x2, blocking collectives: 49 us -> 60.3 us  [summed_over(): got = lax.all_to_all(parts.astype(wire), axis, 0, 0, tiled=True)]
  transfers between devices with their start and end apart: 4 -> 4, of which waited for: 2 -> 2; matrix products, arithmetic and copies ran while one was open for 15% -> 14% of each run, Pallas kernels for 0% -> 0%
where the time goes in v9:
time: 159 us; the launch traced here: 158 us
  blocking collectives  71.5 us (45%)
  waiting for transfers between devices  31.7 us (20%)
  local copies, waits for them, and re-layouts  23.3 us (15%)
  starting transfers between devices  21.2 us (13%)
  matrix products  4.99 us (3%)
  other arithmetic  4.6 us (3%)
    all_to_all x2, blocking collectives, summed_over(): got = lax.all_to_all(parts.astype(wire), axis, 0, 0, tiled=True)  60.3 us
    all_to_all x3, waiting for transfers between devices, spread_to(): lax.all_to_all(jnp.broadcast_to(block[None], (count,) + block.shape), axi...  31.7 us
    all_to_all x3, starting transfers between devices, spread_to(): lax.all_to_all(jnp.broadcast_to(block[None], (count,) + block.shape), axi...  17.4 us
    unnamed x13, local copies, waits for them, and re-layouts  13.9 us
    all_to_all x1, blocking collectives, spread_to(): lax.all_to_all(jnp.broadcast_to(block[None], (count,) + block.shape), axi...  7.37 us
    all_to_all x1, blocking collectives, project_out(): inputs_pair = lax.all_to_all(both, 'core', 0, 0, tiled=True)  3.84 us
    all_to_all x1, starting transfers between devices, pair_rows(): return lax.all_to_all(split, 'core', 0, 0, tiled=True)  3.76 us
    broadcast_in_dim x4, local copies, waits for them, and re-layouts, spread_to(): jnp.broadcast_to(block[None], (count,) + block.shape)  3.71 us
  transfers between devices with their start and end apart: 4, of which 2 were waited for; matrix products, arithmetic and copies ran while one was open for 14% of the time, Pallas kernels for 0%

profile of v9, /device:TPU:24, one launch (start us, length us, event | category | flops | bytes accessed | tf_op | source)
XLA Modules:
  0.0 157.7 jit_solution(14896775749564041541)
XLA Ops:
  0.0 0.9 copy.78
  0.9 0.8 broadcast_in_dim.56
  1.8 8.5 %all-to-all-start = ((bf16[8,256,128]{1,2,0:T(8,128)(2,1)}), bf16[8,256,128]{1,2,0:T(8,128)(2,1)S(1)}, u32[]{:S(2)}, u32[]{:S(2)}) async-start(bf16[8,256,128]{1,2,0:T(8,128)(2,1)} %broadcast_in_dim.56), calls=%async_computation | async-start | bytes 1048576 | tf_op jit(solution)/shard_map/all_to_all | solution.py:22
  10.3 0.7 multiply_negate_fusion
  11.0 16.8 %all-to-all-done = bf16[8,256,128]{1,2,0:T(8,128)(2,1)S(1)} async-done(((bf16[8,256,128]{1,2,0:T(8,128)(2,1)}), bf16[8,256,128]{1,2,0:T(8,128)(2,1)S(1)}, u32[]{:S(2)}, u32[]{:S(2)}) %all-to-all-start) | async-done | bytes 524320 | tf_op jit(solution)/shard_map/all_to_all | solution.py:22
  27.7 1.6 %broadcast_in_dim.57 = bf16[4,8,256,128]{2,3,1,0:T(8,128)(2,1)} broadcast(bf16[8,256,128]{1,2,0:T(8,128)(2,1)S(1)} %all-to-all-done), dimensions={1,2,3} | broadcast | bytes 2621440 | tf_op jit(solution)/shard_map/broadcast_in_dim | solution.py:22
  29.3 4.3 %all-to-all-start.1 = ((bf16[4,8,256,128]{2,3,1,0:T(8,128)(2,1)}), bf16[4,8,256,128]{2,3,1,0:T(8,128)(2,1)S(1)}, u32[]{:S(2)}, u32[]{:S(2)}) async-start(bf16[4,8,256,128]{2,3,1,0:T(8,128)(2,1)} %broadcast_in_dim.57), calls=%async_computation.1 | async-start | bytes 4194304 | tf_op jit(solution)/shard_map/all_to_all | solution.py:22
  33.6 8.6 %copy.80 = bf16[8192,3,128]{0,2,1:T(8,128)(2,1)} copy(bf16[8192,3,128]{2,0,1:T(8,128)(2,1)} %param.7) | data formatting | bytes 12582912 | tf_op args[1]
  43.2 2.0 %multiply_reduce_fusion = f32[8,128,128]{2,1,0:T(8,128)S(1)} fusion(f32[128,128]{1,0:T(8,128)S(1)} %maximum_convert_fusion, f32[16,8]{1,0:T(8,128)S(1)} %copy.89, f32[16,8]{1,0:T(8,128)S(1)} %copy.88), kind=kLoop, calls=%fused_computation | loop fusion | flops 6160384 | bytes 590848 | tf_op jit(solution)/shard_map/reduce_sum | solution.py:162
  45.1 15.0 %all-to-all-done.1 = bf16[4,8,256,128]{2,3,1,0:T(8,128)(2,1)S(1)} async-done(((bf16[4,8,256,128]{2,3,1,0:T(8,128)(2,1)}), bf16[4,8,256,128]{2,3,1,0:T(8,128)(2,1)S(1)}, u32[]{:S(2)}, u32[]{:S(2)}) %all-to-all-start.1) | async-done | bytes 2097184 | tf_op jit(solution)/shard_map/all_to_all | solution.py:22
  60.1 0.7 broadcast_in_dim.58
  60.8 7.4 %all_to_all.40 = bf16[2,4,8,256,128]{3,4,2,1,0:T(8,128)(2,1)S(1)} all-to-all(bf16[2,4,8,256,128]{3,4,2,1,0:T(8,128)(2,1)S(1)} %broadcast_in_dim.58), channel_id=1, replica_groups=mesh['seq'=4,'x'=4,'z'=8,'core'=2] {'core'}, dimensions={0} | all-to-all | bytes 8388608 | tf_op jit(solution)/shard_map/all_to_all | solution.py:22
  68.7 1.1 slice-done.1
  69.8 2.4 %fusion.71 = (f32[256,384]{1,0:T(8,128)S(1)}, bf16[256,384]{1,0:T(8,128)(2,1)S(1)}) fusion(bf16[256,8192]{0,1:T(8,128)(2,1)S(1)} %bitcast.88, bf16[8192,384]{0,1:T(8,128)(2,1)S(1)} %bitcast.87), kind=kOutput, calls=%fused_computation.141 | convolution fusion | flops 1610809344 | bytes 11075584 | tf_op jit(solution)/shard_map/dot_general | solution.py:82
  73.7 4.7 %all-to-all-start.3 = ((f32[4,28,128]{2,1,0:T(8,128)}), f32[4,28,128]{2,1,0:T(8,128)S(1)}, u32[]{:S(2)}, u32[]{:S(2)}) async-start(f32[4,28,128]{2,1,0:T(8,128)} %broadcast_in_dim.64), calls=%async_computation.3 | async-start | bytes 131072 | tf_op jit(solution)/shard_map/all_to_all | solution.py:22
  78.7 3.2 %copy.98 = bf16[128,8192]{0,1:T(8,128)(2,1)S(1)} copy(bf16[128,8192]{1,0:T(8,128)(2,1)} %param.11) | data formatting | bytes 4194304 | tf_op args[5]
  82.0 2.7 %copy.99 = bf16[2,128,4,8,128]{4,1,3,2,0:T(8,128)(2,1)} copy(bf16[2,128,4,8,128]{1,4,0,3,2:T(8,128)(2,1)S(1)} %bitcast.84) | data formatting | bytes 4194304 | tf_op jit(solution)/shard_map/transpose | solution.py:40
  84.6 3.8 %all-to-all-start.5 = ((bf16[2,128,4,8,128]{4,1,3,2,0:T(8,128)(2,1)}), bf16[2,128,4,8,128]{4,1,3,2,0:T(8,128)(2,1)S(1)}, u32[]{:S(2)}, u32[]{:S(2)}) async-start(bf16[2,128,4,8,128]{4,1,3,2,0:T(8,128)(2,1)} %copy.99), calls=%async_computation.5 | async-start | bytes 4194304 | tf_op jit(solution)/shard_map/all_to_all | solution.py:41
  90.7 0.9 fusion.1
  91.8 3.8 %all_to_all.41 = bf16[2,256,128]{2,1,0:T(8,128)(2,1)S(1)} all-to-all(bf16[2,256,128]{2,1,0:T(8,128)(2,1)S(1)} %broadcast_in_dim.124), channel_id=1, replica_groups=mesh['seq'=4,'x'=4,'z'=8,'core'=2] {'core'}, dimensions={0} | all-to-all | bytes 262144 | tf_op jit(solution)/shard_map/all_to_all | solution.py:46
  95.7 0.7 fusion
  96.4 29.4 %all_to_all.42 = bf16[4,8,128,256]{2,3,1,0:T(8,128)(2,1)S(1)} all-to-all(bf16[4,8,128,256]{2,3,1,0:T(8,128)(2,1)S(1)} %fusion), channel_id=1, replica_groups=mesh['seq'=4,'x'=4,'z'=8,'core'=2] {'x'}, dimensions={0} | all-to-all | bytes 4194304 | tf_op jit(solution)/shard_map/all_to_all | solution.py:32
  126.1 30.9 %all_to_all.43 = f32[8,128,256]{1,2,0:T(8,128)S(1)} all-to-all(f32[8,128,256]{1,2,0:T(8,128)S(1)} %convert_reduce_fusion), channel_id=1, replica_groups=mesh['seq'=4,'x'=4,'z'=8,'core'=2] {'z'}, dimensions={0} | all-to-all | bytes 2097152 | tf_op jit(solution)/shard_map/all_to_all | solution.py:32
  157.0 0.7 reduce_sum.92
  (92 shorter events, 5.9 us)
Async XLA Ops:
  1.8 26.0 %all-to-all-start = ((bf16[8,256,128]{1,2,0:T(8,128)(2,1)}), bf16[8,256,128]{1,2,0:T(8,128)(2,1)S(1)}, u32[]{:S(2)}, u32[]{:S(2)}) async-start(bf16[8,256,128]{1,2,0:T(8,128)(2,1)} %broadcast_in_dim.56), calls=%async_computation | async-start | bytes 1048576 | tf_op jit(solution)/shard_map/all_to_all | solution.py:22
  29.3 30.8 %all-to-all-start.1 = ((bf16[4,8,256,128]{2,3,1,0:T(8,128)(2,1)}), bf16[4,8,256,128]{2,3,1,0:T(8,128)(2,1)S(1)}, u32[]{:S(2)}, u32[]{:S(2)}) async-start(bf16[4,8,256,128]{2,3,1,0:T(8,128)(2,1)} %broadcast_in_dim.57), calls=%async_computation.1 | async-start | bytes 4194304 | tf_op jit(solution)/shard_map/all_to_all | solution.py:22
  33.6 9.2 %copy-start = (f32[16,8]{0,1:T(8,128)S(1)}, f32[16,8]{0,1:T(8,128)}, u32[]{:S(2)}) copy-start(f32[16,8]{0,1:T(8,128)} %param.10) | copy-start | bytes 1540
  33.6 9.4 %copy-start.1 = (f32[3,3,128]{2,1,0:T(4,128)S(1)}, f32[3,3,128]{2,1,0:T(4,128)}, u32[]{:S(2)}) copy-start(f32[3,3,128]{2,1,0:T(4,128)} %param.8) | copy-start | bytes 13828
  60.8 7.9 %slice-start = ((s8[6291456]{0:T(1024)(128)(4,1)}), s8[4194304]{0:T(1024)(128)(4,1)S(1)}, s32[]{:S(2)}) async-start(s8[6291456]{0:T(1024)(128)(4,1)} %bitcast.85), calls=%async_computation.8 | async-start | bytes 8388608
  68.2 1.6 %slice-start.1 = ((s8[6291456]{0:T(1024)(128)(4,1)}), s8[2097152]{0:T(1024)(128)(4,1)S(1)}, s32[]{:S(2)}) async-start(s8[6291456]{0:T(1024)(128)(4,1)} %bitcast.85), calls=%async_computation.9 | async-start | bytes 4194304
  73.7 10.9 %all-to-all-start.3 = ((f32[4,28,128]{2,1,0:T(8,128)}), f32[4,28,128]{2,1,0:T(8,128)S(1)}, u32[]{:S(2)}, u32[]{:S(2)}) async-start(f32[4,28,128]{2,1,0:T(8,128)} %broadcast_in_dim.64), calls=%async_computation.3 | async-start | bytes 131072 | tf_op jit(solution)/shard_map/all_to_all | solution.py:22
  84.6 7.2 %all-to-all-start.5 = ((bf16[2,128,4,8,128]{4,1,3,2,0:T(8,128)(2,1)}), bf16[2,128,4,8,128]{4,1,3,2,0:T(8,128)(2,1)S(1)}, u32[]{:S(2)}, u32[]{:S(2)}) async-start(bf16[2,128,4,8,128]{4,1,3,2,0:T(8,128)(2,1)} %copy.99), calls=%async_computation.5 | async-start | bytes 4194304 | tf_op jit(solution)/shard_map/all_to_all | solution.py:41
